TPU v7x, 1024 devices: a whole 4x4x32 slice. The times are simulated.
1024 devices in a mesh: slab: 16 (over z_hi, y, core), dp: 64 (over x, z_lo).
Axes of the slice: x: 4, y: 4, z: 32 (z_hi: 2, z_lo: 16; z = z_hi * 16 + z_lo), core: 2. Of those that a mesh axis runs over, the one named last changes fastest.
Arguments:
- inputs: bfloat16 [64, 32, 24, 64, 128], P('dp', 'slab'), may hold values from -6 to 6
- cotangent: bfloat16 [64, 32, 24, 64, 128], P('dp', 'slab'), may hold values from -4 to 4
- spectral_weight: bfloat16 [16, 256, 4096], P('slab', 'dp'), may hold values from -1.5 to 1.5
- w_in: bfloat16 [64, 256], replicated, may hold values from -0.75 to 0.75
- b_in: float32 [256], replicated, may hold values from -3 to 3
- w_out: bfloat16 [256, 64], replicated, may hold values from -0.375 to 0.375
- b_out: float32 [64], replicated, may hold values from -3 to 3
Outputs:
- grad_inputs: bfloat16 [64, 32, 24, 64, 128], P('dp', 'slab')
- grad_spectral: float32 [16, 256, 4096], P('slab', 'dp')
All inputs are finite; a program needn't handle non-finite values.
Results may differ from a plain program's by a relative error of at most 0.014.
Values may be sent and summed in bfloat16 or wider, within the bound.
No kernel may reach another device: no remote copies, remote signals or barrier semaphores. Data moves between devices by JAX's collectives and lax.ppermute only.
A program may use at most 32 MiB of HBM per device.

v0:
```python
import math

import jax
import jax.numpy as jnp
from jax import lax
from jax.sharding import PartitionSpec as P

C = 64
MX = 16
MY = 16
MZ = 16
NX = 32
NY = 24
NZ = 128


root_half = 0.7071067811865476
inv_root_two_pi = 0.3989422804014327


def dft_table(length, kept_count):
    half_kept = kept_count // 2
    positions = jnp.arange(length, dtype=jnp.int32)
    cos_freq = jnp.arange(half_kept, dtype=jnp.int32)
    freqs = jnp.concatenate([cos_freq, cos_freq + 1])[:, None]
    phases = (freqs * positions[None, :] % length).astype(jnp.float32) * (2.0 * math.pi / length)
    values = jnp.concatenate([jnp.cos(phases[:half_kept]), jnp.sin(phases[half_kept:])], axis=0)
    return values.astype(jnp.bfloat16)


def gelu_value(values_in):
    return 0.5 * values_in * (1.0 + jax.scipy.special.erf(values_in * root_half))


def gelu_slope(values_in):
    return (
        0.5 * (1.0 + jax.scipy.special.erf(values_in * root_half))
        + values_in * jnp.exp(-0.5 * values_in * values_in) * inv_root_two_pi
    )


def bdot(form, left, right):
    return jnp.einsum(form, left, right, preferred_element_type=jnp.float32)


def per_device(inputs, cotangent, spectral_weight, w_in, b_in, w_out, b_out):
    slab_count = lax.axis_size("slab")
    group_count = lax.axis_size("dp")
    local_modes = MY // slab_count
    group_modes = MX * MZ // group_count
    crop_count = inputs.shape[0]
    table_x = dft_table(NX, MX)
    table_y = dft_table(NY, MY)
    table_z = dft_table(NZ, MZ)
    factor = 8.0 / (NX * NY * NZ)

    def analyse(samples):
        along_z = bdot("bxycz,kz->bxyck", samples, table_z).astype(jnp.bfloat16)
        along_y = bdot("bxyck,jy->bxjck", along_z, table_y).astype(jnp.bfloat16)
        return bdot(
            "bxjck,ix->bijck",
            lax.all_to_all(along_y, "slab", split_axis=2, concat_axis=1, tiled=True),
            table_x,
        ).astype(jnp.bfloat16)

    def synthesise(coeff_in):
        back_x = bdot("bijck,ix->bxjck", coeff_in, table_x).astype(jnp.bfloat16)
        back_y = bdot(
            "bxjck,jy->bxyck",
            lax.all_to_all(back_x, "slab", split_axis=1, concat_axis=2, tiled=True),
            table_y,
        ).astype(jnp.bfloat16)
        return bdot("bxyck,kz->bxycz", back_y, table_z) * factor

    def send_out(coeff_in):
        ordered = jnp.transpose(coeff_in, (0, 2, 1, 4, 3)).reshape(
            crop_count, local_modes, group_count, group_modes, C
        )
        arrived = lax.all_to_all(ordered, "dp", split_axis=2, concat_axis=0, tiled=True)
        return arrived.reshape(crop_count * group_count, local_modes, group_modes, C)

    coeffs = analyse(inputs)
    gathered = lax.all_gather(spectral_weight, "dp", axis=1, tiled=True).reshape(
        local_modes, MX, MZ, C, C
    )
    mixed_modes = bdot("bijck,jikco->bijok", coeffs, gathered).astype(jnp.bfloat16)
    spectral = synthesise(mixed_modes)
    activation = bdot("bxycz,ch->bxyhz", inputs, w_in) + b_in[:, None]
    hidden = gelu_value(activation).astype(jnp.bfloat16)
    pre_gelu = bdot("bxyhz,hc->bxycz", hidden, w_out) + b_out[:, None] + spectral
    grad_pre = (cotangent.astype(jnp.float32) * gelu_slope(pre_gelu)).astype(jnp.bfloat16)
    grad_act = (bdot("bxycz,hc->bxyhz", grad_pre, w_out) * gelu_slope(activation)).astype(
        jnp.bfloat16
    )
    grad_coeffs = analyse(grad_pre)
    back_modes = bdot("bijok,jikco->bijck", grad_coeffs, gathered).astype(jnp.bfloat16)
    routed = send_out(coeffs)
    grad_routed = send_out(grad_coeffs)
    grad_weight = (bdot("bjgc,bjgo->jgco", routed, grad_routed) * factor).reshape(
        local_modes, group_modes, C * C
    )
    grad_field = (bdot("bxyhz,ch->bxycz", grad_act, w_in) + synthesise(back_modes)).astype(
        jnp.bfloat16
    )
    return (grad_field, grad_weight)


def solution(mesh):
    return jax.shard_map(
        per_device,
        mesh=mesh,
        in_specs=(
            P("dp", "slab", None, None, None),
            P("dp", "slab", None, None, None),
            P("slab", "dp", None),
            P(),
            P(),
            P(),
            P(),
        ),
        out_specs=(P("dp", "slab", None, None, None), P("slab", "dp", None)),
        check_vma=False,
    )
```

profile of v0, /device:TPU:1, one launch (start us, length us, event | category | flops | bytes accessed | tf_op | source)
XLA Modules:
  0.0 942.6 jit_solution(2737668892400223272)
XLA Ops:
  7.2 1.5 copy.48
  10.1 0.8 reshape.162
  10.9 32.5 %all-to-all-start = ((bf16[16,2,1024]{2,1,0:T(2,128)(2,1)}), bf16[16,2,1024]{2,1,0:T(2,128)(2,1)S(1)}, u32[]{:S(2)}, u32[]{:S(2)}) async-start(bf16[16,2,1024]{2,1,0:T(2,128)(2,1)} %reshape.162), calls=%async_computation | async-start | bytes 131072 | tf_op jit(solution)/shard_map/all_to_all | solution.py:62
  43.5 24.0 %all-to-all-done = bf16[16,2,1024]{2,1,0:T(2,128)(2,1)S(1)} async-done(((bf16[16,2,1024]{2,1,0:T(2,128)(2,1)}), bf16[16,2,1024]{2,1,0:T(2,128)(2,1)S(1)}, u32[]{:S(2)}, u32[]{:S(2)}) %all-to-all-start) | async-done | bytes 65568 | tf_op jit(solution)/shard_map/all_to_all | solution.py:62
  67.8 628.1 %all-gather.2.cloned.1.call-done = bf16[1,256,4096]{2,0,1:T(2,128)(2,1)} async-done(((bf16[1,4,4096]{2,0,1:T(2,128)(2,1)}), bf16[1,256,4096]{2,0,1:T(2,128)(2,1)}) %all-gather.2.cloned.1.call-update) | async-done | bytes 2097168 | tf_op jit(solution)/shard_map/all_gather | solution.py:83
  695.9 12.9 %reduce = bf16[256,4096]{1,0:T(8,128)(2,1)S(1)} reduce(bf16[1,256,4096]{2,0,1:T(2,128)(2,1)} %all-gather.2.cloned.1.call-done, bf16[]{:T(256)} %constant.69), dimensions={0}, to_apply=%all_gather.3.reduce_sub_computation | reduce | bytes 4194306 | tf_op jit(solution)/shard_map/all_gather | solution.py:83
  708.8 5.5 reshape.137
  714.3 3.4 fusion.57
  718.0 0.8 reshape.164
  718.8 63.7 %all-to-all-start.1 = ((bf16[16,2,1024]{2,1,0:T(2,128)(2,1)}), bf16[16,2,1024]{2,1,0:T(2,128)(2,1)S(1)}, u32[]{:S(2)}, u32[]{:S(2)}) async-start(bf16[16,2,1024]{2,1,0:T(2,128)(2,1)} %reshape.164), calls=%async_computation.1 | async-start | bytes 131072 | tf_op jit(solution)/shard_map/all_to_all | solution.py:70
  782.5 3.7 fusion.45
  786.2 20.4 %all-to-all-done.1 = bf16[16,2,1024]{2,1,0:T(2,128)(2,1)S(1)} async-done(((bf16[16,2,1024]{2,1,0:T(2,128)(2,1)}), bf16[16,2,1024]{2,1,0:T(2,128)(2,1)S(1)}, u32[]{:S(2)}, u32[]{:S(2)}) %all-to-all-start.1) | async-done | bytes 65568 | tf_op jit(solution)/shard_map/all_to_all | solution.py:70
  807.5 4.4 fusion.34
  812.9 0.8 reshape.166
  813.7 3.7 all-to-all-start.2
  818.1 23.5 %all-to-all-done.2 = bf16[16,2,1024]{2,1,0:T(2,128)(2,1)S(1)} async-done(((bf16[16,2,1024]{2,1,0:T(2,128)(2,1)}), bf16[16,2,1024]{2,1,0:T(2,128)(2,1)S(1)}, u32[]{:S(2)}, u32[]{:S(2)}) %all-to-all-start.2) | async-done | bytes 65568 | tf_op jit(solution)/shard_map/all_to_all | solution.py:62
  841.6 9.1 all-to-all-start.4
  851.7 19.8 %all-to-all-done.4 = bf16[64,2,128]{2,1,0:T(2,128)(2,1)S(1)} async-done(((bf16[64,2,128]{2,1,0:T(2,128)(2,1)}), bf16[64,2,128]{2,1,0:T(2,128)(2,1)S(1)}, u32[]{:S(2)}, u32[]{:S(2)}) %all-to-all-start.4) | async-done | bytes 32800 | tf_op jit(solution)/shard_map/all_to_all | solution.py:79
  871.5 5.7 all-to-all-start.5
  877.2 4.4 fusion.55
  882.8 15.1 %all-to-all-done.5 = bf16[64,2,128]{2,1,0:T(2,128)(2,1)S(1)} async-done(((bf16[64,2,128]{2,1,0:T(2,128)(2,1)}), bf16[64,2,128]{2,1,0:T(2,128)(2,1)S(1)}, u32[]{:S(2)}, u32[]{:S(2)}) %all-to-all-start.5) | async-done | bytes 32800 | tf_op jit(solution)/shard_map/all_to_all | solution.py:79
  897.9 5.6 all-to-all-start.3
  904.6 23.0 %all-to-all-done.3 = bf16[16,2,1024]{2,1,0:T(2,128)(2,1)S(1)} async-done(((bf16[16,2,1024]{2,1,0:T(2,128)(2,1)}), bf16[16,2,1024]{2,1,0:T(2,128)(2,1)S(1)}, u32[]{:S(2)}, u32[]{:S(2)}) %all-to-all-start.3) | async-done | bytes 65568 | tf_op jit(solution)/shard_map/all_to_all | solution.py:70
  928.5 7.3 fusion.27
  (53 shorter events, 8.6 us)
Async XLA Ops:
  7.2 2.0 copy-start
  7.2 688.7 %all-gather.2.cloned.1.call-start = ((), (), s32[]{:S(2)}) async-start(), calls=%async_computation.6 | async-start | bytes 4259840 | tf_op jit(solution)/shard_map/all_gather | solution.py:83
  10.9 56.6 %all-to-all-start = ((bf16[16,2,1024]{2,1,0:T(2,128)(2,1)}), bf16[16,2,1024]{2,1,0:T(2,128)(2,1)S(1)}, u32[]{:S(2)}, u32[]{:S(2)}) async-start(bf16[16,2,1024]{2,1,0:T(2,128)(2,1)} %reshape.162), calls=%async_computation | async-start | bytes 131072 | tf_op jit(solution)/shard_map/all_to_all | solution.py:62
  714.3 68.2 %copy-start.1 = (bf16[64,256]{1,0:T(8,128)(2,1)S(1)}, bf16[64,256]{1,0:T(8,128)(2,1)}, u32[]{:S(2)}) copy-start(bf16[64,256]{1,0:T(8,128)(2,1)} %param.10) | copy-start | bytes 98308
  718.8 87.9 %all-to-all-start.1 = ((bf16[16,2,1024]{2,1,0:T(2,128)(2,1)}), bf16[16,2,1024]{2,1,0:T(2,128)(2,1)S(1)}, u32[]{:S(2)}, u32[]{:S(2)}) async-start(bf16[16,2,1024]{2,1,0:T(2,128)(2,1)} %reshape.164), calls=%async_computation.1 | async-start | bytes 131072 | tf_op jit(solution)/shard_map/all_to_all | solution.py:70
  782.5 25.0 %copy-start.2 = (bf16[1,2,24,64,128]{4,3,2,1,0:T(8,128)(2,1)S(1)}, bf16[1,2,24,64,128]{4,3,2,1,0:T(8,128)(2,1)}, u32[]{:S(2)}) copy-start(bf16[1,2,24,64,128]{4,3,2,1,0:T(8,128)(2,1)} %param.8) | copy-start | bytes 2359300
  782.5 25.0 %copy-start.3 = (bf16[256,64]{0,1:T(8,128)(2,1)S(1)}, bf16[256,64]{0,1:T(8,128)(2,1)}, u32[]{:S(2)}) copy-start(bf16[256,64]{0,1:T(8,128)(2,1)} %param.12) | copy-start | bytes 98308
  782.5 25.0 %copy-start.4 = (f32[256]{0:T(256)S(1)}, f32[256]{0:T(256)}, u32[]{:S(2)}) copy-start(f32[256]{0:T(256)} %param.11) | copy-start | bytes 3076
  782.5 25.0 %copy-start.5 = (f32[64]{0:T(128)S(1)}, f32[64]{0:T(128)}, u32[]{:S(2)}) copy-start(f32[64]{0:T(128)} %param.13) | copy-start | bytes 772
  813.7 28.0 %all-to-all-start.2 = ((bf16[16,2,1024]{2,1,0:T(2,128)(2,1)}), bf16[16,2,1024]{2,1,0:T(2,128)(2,1)S(1)}, u32[]{:S(2)}, u32[]{:S(2)}) async-start(bf16[16,2,1024]{2,1,0:T(2,128)(2,1)} %reshape.166), calls=%async_computation.2 | async-start | bytes 131072 | tf_op jit(solution)/shard_map/all_to_all | solution.py:62
  841.6 29.9 %all-to-all-start.4 = ((bf16[64,2,128]{2,1,0:T(2,128)(2,1)}), bf16[64,2,128]{2,1,0:T(2,128)(2,1)S(1)}, u32[]{:S(2)}, u32[]{:S(2)}) async-start(bf16[64,2,128]{2,1,0:T(2,128)(2,1)} %reshape.170), calls=%async_computation.4 | async-start | bytes 65536 | tf_op jit(solution)/shard_map/all_to_all | solution.py:79
  871.5 26.4 %all-to-all-start.5 = ((bf16[64,2,128]{2,1,0:T(2,128)(2,1)}), bf16[64,2,128]{2,1,0:T(2,128)(2,1)S(1)}, u32[]{:S(2)}, u32[]{:S(2)}) async-start(bf16[64,2,128]{2,1,0:T(2,128)(2,1)} %reshape.172), calls=%async_computation.5 | async-start | bytes 65536 | tf_op jit(solution)/shard_map/all_to_all | solution.py:79
  897.9 29.8 %all-to-all-start.3 = ((bf16[16,2,1024]{2,1,0:T(2,128)(2,1)}), bf16[16,2,1024]{2,1,0:T(2,128)(2,1)S(1)}, u32[]{:S(2)}, u32[]{:S(2)}) async-start(bf16[16,2,1024]{2,1,0:T(2,128)(2,1)} %reshape.168), calls=%async_computation.3 | async-start | bytes 131072 | tf_op jit(solution)/shard_map/all_to_all | solution.py:70
Sparse Core Ops, SparseCore 0:
  11.2 684.6 all-gather.1
where the time goes:
time: 946 us; the launch traced here: 943 us
  waiting for transfers between devices  754 us (80%)
  starting transfers between devices  120 us (13%)
  matrix products  27.2 us (3%)
  between operations  14.3 us (2%)
  local copies, waits for them, and re-layouts  13.4 us (1%)
  other arithmetic  13.4 us (1%)
    all_gather x1, waiting for transfers between devices, per_device(): lax.all_gather(spectral_weight, 'dp', axis=1, tiled=True)  628 us
    all_to_all x2, starting transfers between devices, synthesise(): lax.all_to_all(back_x, 'slab', split_axis=1, concat_axis=2, tiled=True)  69.3 us
    all_to_all x2, waiting for transfers between devices, analyse(): lax.all_to_all(along_y, 'slab', split_axis=2, concat_axis=1, tiled=True)  47.5 us
    all_to_all x2, waiting for transfers between devices, synthesise(): lax.all_to_all(back_x, 'slab', split_axis=1, concat_axis=2, tiled=True)  43.5 us
    all_to_all x2, starting transfers between devices, analyse(): lax.all_to_all(along_y, 'slab', split_axis=2, concat_axis=1, tiled=True)  36.2 us
    all_to_all x2, waiting for transfers between devices, send_out(): lax.all_to_all(ordered, 'dp', split_axis=2, concat_axis=0, tiled=True)  34.9 us
    dot_general x18, matrix products, bdot(): return jnp.einsum(form, left, right, preferred_element_type=jnp.float32)  27.2 us
  transfers between devices with their start and end apart: 7, of which 7 were waited for; matrix products, arithmetic and copies ran while one was open for 2% of the time, Pallas kernels for 0%

commit v1 on v0

--- a/solution.py
+++ b/solution.py
@@ -79,11 +79,20 @@
         arrived = lax.all_to_all(ordered, "dp", split_axis=2, concat_axis=0, tiled=True)
         return arrived.reshape(crop_count * group_count, local_modes, group_modes, C)
 
+    def send_back(routed_in):
+        returned = lax.all_to_all(
+            routed_in.reshape(crop_count * group_count, local_modes, 1, group_modes, C),
+            "dp", split_axis=0, concat_axis=2, tiled=True,
+        )
+        return jnp.transpose(
+            returned.reshape(crop_count, local_modes, MX, MZ, C), (0, 2, 1, 4, 3)
+        )
+
+    weights = spectral_weight.reshape(local_modes, group_modes, C, C)
     coeffs = analyse(inputs)
-    gathered = lax.all_gather(spectral_weight, "dp", axis=1, tiled=True).reshape(
-        local_modes, MX, MZ, C, C
-    )
-    mixed_modes = bdot("bijck,jikco->bijok", coeffs, gathered).astype(jnp.bfloat16)
+    routed = send_out(coeffs)
+    mixed_routed = bdot("bjgc,jgco->bjgo", routed, weights).astype(jnp.bfloat16)
+    mixed_modes = send_back(mixed_routed)
     spectral = synthesise(mixed_modes)
     activation = bdot("bxycz,ch->bxyhz", inputs, w_in) + b_in[:, None]
     hidden = gelu_value(activation).astype(jnp.bfloat16)
@@ -93,9 +102,9 @@
         jnp.bfloat16
     )
     grad_coeffs = analyse(grad_pre)
-    back_modes = bdot("bijok,jikco->bijck", grad_coeffs, gathered).astype(jnp.bfloat16)
-    routed = send_out(coeffs)
     grad_routed = send_out(grad_coeffs)
+    back_routed = bdot("bjgo,jgco->bjgc", grad_routed, weights).astype(jnp.bfloat16)
+    back_modes = send_back(back_routed)
     grad_weight = (bdot("bjgc,bjgo->jgco", routed, grad_routed) * factor).reshape(
         local_modes, group_modes, C * C
     )

time: 946 us -> 284 us (0.30)
  waiting for transfers between devices: 754 us -> 87.7 us
  blocking collectives: 0 us -> 109 us
  starting transfers between devices: 120 us -> 55.5 us
  between operations: 14.3 us -> 0.95 us
  other arithmetic: 13.4 us -> 0.48 us
    all_gather x1 -> x0, waiting for transfers between devices: 628 us -> none  [per_device(): lax.all_gather(spectral_weight, 'dp', axis=1, tiled=True)]
    all_to_all x0 -> x4, blocking collectives: none -> 109 us  [the longest x2 52.5 us: send_back(): lax.all_to_all(routed_in.reshape(crop_count * group_count, local_modes, 1...]
    all_to_all x2, starting transfers between devices: 69.3 us -> 11.1 us  [synthesise(): lax.all_to_all(back_x, 'slab', split_axis=1, concat_axis=2, tiled=True)]
    all_to_all x2 -> x1, waiting for transfers between devices: 47.5 us -> 24 us  [analyse(): lax.all_to_all(along_y, 'slab', split_axis=2, concat_axis=1, tiled=True)]
    all_to_all x2 -> x1, waiting for transfers between devices: 34.9 us -> 19.9 us  [send_out(): lax.all_to_all(ordered, 'dp', split_axis=2, concat_axis=0, tiled=True)]
    all_gather x1 -> x0, other arithmetic: 12.9 us -> none  [per_device(): lax.all_gather(spectral_weight, 'dp', axis=1, tiled=True)]
    all_to_all x2 -> x1, starting transfers between devices: 36.2 us -> 32.5 us  [analyse(): lax.all_to_all(along_y, 'slab', split_axis=2, concat_axis=1, tiled=True)]
  transfers between devices with their start and end apart: 7 -> 4, of which waited for: 7 -> 4; matrix products, arithmetic and copies ran while one was open for 2% -> 2% of each run, Pallas kernels for 0% -> 0%
where the time goes in v1:
time: 284 us; the launch traced here: 281 us
  blocking collectives  109 us (38%)
  waiting for transfers between devices  87.7 us (31%)
  starting transfers between devices  55.5 us (20%)
  matrix products  19.7 us (7%)
  local copies, waits for them, and re-layouts  7.07 us (2%)
    all_to_all x2, blocking collectives, send_back(): lax.all_to_all(routed_in.reshape(crop_count * group_count, local_modes, 1...  52.5 us
    all_to_all x2, waiting for transfers between devices, synthesise(): lax.all_to_all(back_x, 'slab', split_axis=1, concat_axis=2, tiled=True)  43.8 us
    all_to_all x1, starting transfers between devices, analyse(): lax.all_to_all(along_y, 'slab', split_axis=2, concat_axis=1, tiled=True)  32.5 us
    all_to_all x1, blocking collectives, send_out(): lax.all_to_all(ordered, 'dp', split_axis=2, concat_axis=0, tiled=True)  29.3 us
    all_to_all x1, blocking collectives, analyse(): lax.all_to_all(along_y, 'slab', split_axis=2, concat_axis=1, tiled=True)  27.6 us
    all_to_all x1, waiting for transfers between devices, analyse(): lax.all_to_all(along_y, 'slab', split_axis=2, concat_axis=1, tiled=True)  24 us
    all_to_all x1, waiting for transfers between devices, send_out(): lax.all_to_all(ordered, 'dp', split_axis=2, concat_axis=0, tiled=True)  19.9 us
    dot_general x18, matrix products, bdot(): return jnp.einsum(form, left, right, preferred_element_type=jnp.float32)  19.7 us
  transfers between devices with their start and end apart: 4, of which 4 were waited for; matrix products, arithmetic and copies ran while one was open for 2% of the time, Pallas kernels for 0%

profile of v1, /device:TPU:1, one launch (start us, length us, event | category | flops | bytes accessed | tf_op | source)
XLA Modules:
  0.0 280.8 jit_solution(7600707792960527277)
XLA Ops:
  1.0 0.7 copy-done
  1.8 0.7 fusion.37
  2.7 0.8 reshape.181
  3.5 32.5 %all-to-all-start = ((bf16[16,2,1024]{2,1,0:T(2,128)(2,1)}), bf16[16,2,1024]{2,1,0:T(2,128)(2,1)S(1)}, u32[]{:S(2)}, u32[]{:S(2)}) async-start(bf16[16,2,1024]{2,1,0:T(2,128)(2,1)} %reshape.181), calls=%async_computation | async-start | bytes 131072 | tf_op jit(solution)/shard_map/all_to_all | solution.py:62
  36.1 24.0 %all-to-all-done = bf16[16,2,1024]{2,1,0:T(2,128)(2,1)S(1)} async-done(((bf16[16,2,1024]{2,1,0:T(2,128)(2,1)}), bf16[16,2,1024]{2,1,0:T(2,128)(2,1)S(1)}, u32[]{:S(2)}, u32[]{:S(2)}) %all-to-all-start) | async-done | bytes 65568 | tf_op jit(solution)/shard_map/all_to_all | solution.py:62
  60.4 0.7 reshape.183
  61.2 11.9 %all-to-all-start.1 = ((bf16[64,2,128]{2,1,0:T(2,128)(2,1)}), bf16[64,2,128]{2,1,0:T(2,128)(2,1)S(1)}, u32[]{:S(2)}, u32[]{:S(2)}) async-start(bf16[64,2,128]{2,1,0:T(2,128)(2,1)} %reshape.183), calls=%async_computation.1 | async-start | bytes 65536 | tf_op jit(solution)/shard_map/all_to_all | solution.py:79
  73.0 0.9 reshape.159
  73.9 19.9 %all-to-all-done.1 = bf16[64,2,128]{2,1,0:T(2,128)(2,1)S(1)} async-done(((bf16[64,2,128]{2,1,0:T(2,128)(2,1)}), bf16[64,2,128]{2,1,0:T(2,128)(2,1)S(1)}, u32[]{:S(2)}, u32[]{:S(2)}) %all-to-all-start.1) | async-done | bytes 32800 | tf_op jit(solution)/shard_map/all_to_all | solution.py:79
  94.2 26.3 %all_to_all.96 = bf16[64,2,128]{2,1,0:T(2,128)(2,1)S(1)} all-to-all(bf16[64,2,128]{2,1,0:T(2,128)(2,1)S(1)} %reshape.185), channel_id=1, replica_groups=mesh['slab'=16,'dp'=64] {'dp'}, dimensions={0} | all-to-all | bytes 65536 | tf_op jit(solution)/shard_map/all_to_all | solution.py:83
  120.9 0.8 reshape.187
  121.6 5.6 %all-to-all-start.3 = ((bf16[16,2,1024]{2,1,0:T(2,128)(2,1)}), bf16[16,2,1024]{2,1,0:T(2,128)(2,1)S(1)}, u32[]{:S(2)}, u32[]{:S(2)}) async-start(bf16[16,2,1024]{2,1,0:T(2,128)(2,1)} %reshape.187), calls=%async_computation.3 | async-start | bytes 131072 | tf_op jit(solution)/shard_map/all_to_all | solution.py:70
  127.3 3.7 %fusion.49 = f32[256,2,24,128]{3,0,2,1:T(8,128)} fusion(bf16[1,2,24,64,128]{4,3,2,1,0:T(8,128)(2,1)S(1)} %copy-done, bf16[64,256]{1,0:T(8,128)(2,1)S(1)} %copy-done.1), kind=kOutput, calls=%fused_computation.59 | convolution fusion | flops 201326592 | bytes 7110656 | tf_op jit(solution)/shard_map/bxycz,ch->bxyhz/dot_general | solution.py:43
  130.9 20.5 %all-to-all-done.3 = bf16[16,2,1024]{2,1,0:T(2,128)(2,1)S(1)} async-done(((bf16[16,2,1024]{2,1,0:T(2,128)(2,1)}), bf16[16,2,1024]{2,1,0:T(2,128)(2,1)S(1)}, u32[]{:S(2)}, u32[]{:S(2)}) %all-to-all-start.3) | async-done | bytes 65568 | tf_op jit(solution)/shard_map/all_to_all | solution.py:70
  152.3 4.4 %fusion.34 = bf16[2,24,64,128]{3,2,1,0:T(8,128)(2,1)S(1)} fusion(f32[2,24,64,128]{3,2,1,0:T(8,128)S(1)} %fusion.54, f32[256,2,24,128]{3,0,2,1:T(8,128)} %fusion.49, f32[256]{0:T(256)S(1)} %copy-done.4, bf16[1,2,24,64,128]{4,3,2,1,0:T(8,128)(2,1)S(1)} %copy-done.2, f32[64]{0:T(128)S(1)} %copy-done.5, bf16[256,64]{0,1:T(8,128)(2,1)S(1)} %copy-done.3), kind=kOutput, calls=%fused_computation.33 | convolution fusion | flops 216268800 | bytes 9471232 | tf_op jit(solution)/shard_map/bxyhz,hc->bxycz/dot_general | solution.py:43
  156.7 0.7 convolution_convert_fusion.1
  157.8 27.6 %all_to_all.97 = bf16[16,2,1024]{2,1,0:T(2,128)(2,1)S(1)} all-to-all(bf16[16,2,1024]{2,1,0:T(2,128)(2,1)S(1)} %reshape.189), channel_id=1, replica_groups=mesh['slab'=16,'dp'=64] {'slab'}, dimensions={0} | all-to-all | bytes 131072 | tf_op jit(solution)/shard_map/all_to_all | solution.py:62
  185.8 29.3 %all_to_all.98 = bf16[64,2,128]{2,1,0:T(2,128)(2,1)S(1)} all-to-all(bf16[64,2,128]{2,1,0:T(2,128)(2,1)S(1)} %reshape.191), channel_id=1, replica_groups=mesh['slab'=16,'dp'=64] {'dp'}, dimensions={0} | all-to-all | bytes 65536 | tf_op jit(solution)/shard_map/all_to_all | solution.py:79
  215.6 26.3 %all_to_all.99 = bf16[64,2,128]{2,1,0:T(2,128)(2,1)S(1)} all-to-all(bf16[64,2,128]{2,1,0:T(2,128)(2,1)S(1)} %reshape.193), channel_id=1, replica_groups=mesh['slab'=16,'dp'=64] {'dp'}, dimensions={0} | all-to-all | bytes 65536 | tf_op jit(solution)/shard_map/all_to_all | solution.py:83
  242.2 0.8 reshape.195
  243.0 5.6 %all-to-all-start.7 = ((bf16[16,2,1024]{2,1,0:T(2,128)(2,1)}), bf16[16,2,1024]{2,1,0:T(2,128)(2,1)S(1)}, u32[]{:S(2)}, u32[]{:S(2)}) async-start(bf16[16,2,1024]{2,1,0:T(2,128)(2,1)} %reshape.195), calls=%async_computation.7 | async-start | bytes 131072 | tf_op jit(solution)/shard_map/all_to_all | solution.py:70
  248.7 0.7 reshape.175
  249.5 23.3 %all-to-all-done.7 = bf16[16,2,1024]{2,1,0:T(2,128)(2,1)S(1)} async-done(((bf16[16,2,1024]{2,1,0:T(2,128)(2,1)}), bf16[16,2,1024]{2,1,0:T(2,128)(2,1)S(1)}, u32[]{:S(2)}, u32[]{:S(2)}) %all-to-all-start.7) | async-done | bytes 65568 | tf_op jit(solution)/shard_map/all_to_all | solution.py:70
  273.6 7.3 %fusion.27 = bf16[1,2,24,64,128]{4,3,2,1,0:T(8,128)(2,1)} fusion(f32[2,24,64,128]{3,2,1,0:T(8,128)S(1)} %fusion.51, f32[256]{0:T(256)S(1)} %copy-done.4, f32[256,2,24,128]{3,0,2,1:T(8,128)} %fusion.49, bf16[2,24,64,128]{3,2,1,0:T(8,128)(2,1)S(1)} %fusion.34, bf16[256,64]{0,1:T(8,128)(2,1)S(1)} %copy-done.3, bf16[64,256]{1,0:T(8,128)(2,1)S(1)} %copy-done.1), kind=kOutput, calls=%fused_computation.29 | convolution fusion | flops 421134336 | bytes 9503744 | tf_op jit(solution)/shard_map/bxyhz,ch->bxycz/dot_general | solution.py:43
  (53 shorter events, 5.1 us)
Async XLA Ops:
  0.6 1.1 copy-start
  0.6 126.6 %copy-start.1 = (bf16[64,256]{1,0:T(8,128)(2,1)S(1)}, bf16[64,256]{1,0:T(8,128)(2,1)}, u32[]{:S(2)}) copy-start(bf16[64,256]{1,0:T(8,128)(2,1)} %param.10) | copy-start | bytes 98308
  3.5 56.6 %all-to-all-start = ((bf16[16,2,1024]{2,1,0:T(2,128)(2,1)}), bf16[16,2,1024]{2,1,0:T(2,128)(2,1)S(1)}, u32[]{:S(2)}, u32[]{:S(2)}) async-start(bf16[16,2,1024]{2,1,0:T(2,128)(2,1)} %reshape.181), calls=%async_computation | async-start | bytes 131072 | tf_op jit(solution)/shard_map/all_to_all | solution.py:62
  61.2 32.7 %all-to-all-start.1 = ((bf16[64,2,128]{2,1,0:T(2,128)(2,1)}), bf16[64,2,128]{2,1,0:T(2,128)(2,1)S(1)}, u32[]{:S(2)}, u32[]{:S(2)}) async-start(bf16[64,2,128]{2,1,0:T(2,128)(2,1)} %reshape.183), calls=%async_computation.1 | async-start | bytes 65536 | tf_op jit(solution)/shard_map/all_to_all | solution.py:79
  121.6 29.8 %all-to-all-start.3 = ((bf16[16,2,1024]{2,1,0:T(2,128)(2,1)}), bf16[16,2,1024]{2,1,0:T(2,128)(2,1)S(1)}, u32[]{:S(2)}, u32[]{:S(2)}) async-start(bf16[16,2,1024]{2,1,0:T(2,128)(2,1)} %reshape.187), calls=%async_computation.3 | async-start | bytes 131072 | tf_op jit(solution)/shard_map/all_to_all | solution.py:70
  127.2 25.0 %copy-start.2 = (bf16[1,2,24,64,128]{4,3,2,1,0:T(8,128)(2,1)S(1)}, bf16[1,2,24,64,128]{4,3,2,1,0:T(8,128)(2,1)}, u32[]{:S(2)}) copy-start(bf16[1,2,24,64,128]{4,3,2,1,0:T(8,128)(2,1)} %param.8) | copy-start | bytes 2359300
  127.2 25.0 %copy-start.3 = (bf16[256,64]{0,1:T(8,128)(2,1)S(1)}, bf16[256,64]{0,1:T(8,128)(2,1)}, u32[]{:S(2)}) copy-start(bf16[256,64]{0,1:T(8,128)(2,1)} %param.12) | copy-start | bytes 98308
  127.2 25.0 %copy-start.4 = (f32[256]{0:T(256)S(1)}, f32[256]{0:T(256)}, u32[]{:S(2)}) copy-start(f32[256]{0:T(256)} %param.11) | copy-start | bytes 3076
  127.2 25.0 %copy-start.5 = (f32[64]{0:T(128)S(1)}, f32[64]{0:T(128)}, u32[]{:S(2)}) copy-start(f32[64]{0:T(128)} %param.13) | copy-start | bytes 772
  243.0 29.8 %all-to-all-start.7 = ((bf16[16,2,1024]{2,1,0:T(2,128)(2,1)}), bf16[16,2,1024]{2,1,0:T(2,128)(2,1)S(1)}, u32[]{:S(2)}, u32[]{:S(2)}) async-start(bf16[16,2,1024]{2,1,0:T(2,128)(2,1)} %reshape.195), calls=%async_computation.7 | async-start | bytes 131072 | tf_op jit(solution)/shard_map/all_to_all | solution.py:70

commit v2 on v1

--- a/solution.py
+++ b/solution.py
@@ -3,7 +3,7 @@
 import jax
 import jax.numpy as jnp
 from jax import lax
-from jax.sharding import PartitionSpec as P
+from jax.sharding import Mesh, PartitionSpec as P
 
 C = 64
 MX = 16
@@ -44,7 +44,9 @@
 
 
 def per_device(inputs, cotangent, spectral_weight, w_in, b_in, w_out, b_out):
-    slab_count = lax.axis_size("slab")
+    outer_count = lax.axis_size("zh")
+    inner_count = lax.axis_size("yc")
+    slab_count = outer_count * inner_count
     group_count = lax.axis_size("dp")
     local_modes = MY // slab_count
     group_modes = MX * MZ // group_count
@@ -54,22 +56,28 @@
     table_z = dft_table(NZ, MZ)
     factor = 8.0 / (NX * NY * NZ)
 
+    def gather_x(local):
+        b_, xl, nj, c_, k_ = local.shape
+        local = local.reshape(b_, xl, outer_count, inner_count, c_, k_)
+        local = jnp.transpose(local, (0, 1, 3, 2, 4, 5)).reshape(b_, xl, nj, c_, k_)
+        local = lax.all_to_all(local, "yc", split_axis=2, concat_axis=1, tiled=True)
+        return lax.all_to_all(local, "zh", split_axis=2, concat_axis=1, tiled=True)
+
+    def scatter_x(whole):
+        whole = lax.all_to_all(whole, "zh", split_axis=1, concat_axis=2, tiled=True)
+        whole = lax.all_to_all(whole, "yc", split_axis=1, concat_axis=2, tiled=True)
+        b_, xl, nj, c_, k_ = whole.shape
+        whole = whole.reshape(b_, xl, inner_count, outer_count, c_, k_)
+        return jnp.transpose(whole, (0, 1, 3, 2, 4, 5)).reshape(b_, xl, nj, c_, k_)
+
     def analyse(samples):
         along_z = bdot("bxycz,kz->bxyck", samples, table_z).astype(jnp.bfloat16)
         along_y = bdot("bxyck,jy->bxjck", along_z, table_y).astype(jnp.bfloat16)
-        return bdot(
-            "bxjck,ix->bijck",
-            lax.all_to_all(along_y, "slab", split_axis=2, concat_axis=1, tiled=True),
-            table_x,
-        ).astype(jnp.bfloat16)
+        return bdot("bxjck,ix->bijck", gather_x(along_y), table_x).astype(jnp.bfloat16)
 
     def synthesise(coeff_in):
         back_x = bdot("bijck,ix->bxjck", coeff_in, table_x).astype(jnp.bfloat16)
-        back_y = bdot(
-            "bxjck,jy->bxyck",
-            lax.all_to_all(back_x, "slab", split_axis=1, concat_axis=2, tiled=True),
-            table_y,
-        ).astype(jnp.bfloat16)
+        back_y = bdot("bxjck,jy->bxyck", scatter_x(back_x), table_y).astype(jnp.bfloat16)
         return bdot("bxyck,kz->bxycz", back_y, table_z) * factor
 
     def send_out(coeff_in):
@@ -115,18 +123,25 @@
 
 
 def solution(mesh):
+    slab_size = mesh.shape["slab"]
+    inner_size = 8 if slab_size % 8 == 0 else slab_size
+    split_mesh = Mesh(
+        mesh.devices.reshape(slab_size // inner_size, inner_size, mesh.shape["dp"]),
+        ("zh", "yc", "dp"),
+    )
+    slab = ("zh", "yc")
     return jax.shard_map(
         per_device,
-        mesh=mesh,
+        mesh=split_mesh,
         in_specs=(
-            P("dp", "slab", None, None, None),
-            P("dp", "slab", None, None, None),
-            P("slab", "dp", None),
+            P("dp", slab, None, None, None),
+            P("dp", slab, None, None, None),
+            P(slab, "dp", None),
             P(),
             P(),
             P(),
             P(),
         ),
-        out_specs=(P("dp", "slab", None, None, None), P("slab", "dp", None)),
+        out_specs=(P("dp", slab, None, None, None), P(slab, "dp", None)),
         check_vma=False,
     )

time: 284 us -> 305 us (1.074)
  blocking collectives: 109 us -> 181 us
  waiting for transfers between devices: 87.7 us -> 47.3 us
  starting transfers between devices: 55.5 us -> 46.1 us
    all_to_all x1 -> x5, blocking collectives: 27.6 us -> 101 us  [the longest x2 47.6 us: scatter_x(): whole = lax.all_to_all(whole, 'zh', split_axis=1, concat_axis=2, tiled=True)]
    all_to_all x3, waiting for transfers between devices: 67.8 us -> 26.6 us  [the longest x1 21.5 us: gather_x(): return lax.all_to_all(local, 'zh', split_axis=2, concat_axis=1, tiled=True)]
    all_to_all x3, starting transfers between devices: 43.6 us -> 34.3 us  [the longest x1 17.3 us: gather_x(): return lax.all_to_all(local, 'zh', split_axis=2, concat_axis=1, tiled=True)]
    unnamed x28 -> x38, local copies, waits for them, and re-layouts: 5.12 us -> 6.44 us
where the time goes in v2:
time: 305 us; the launch traced here: 304 us
  blocking collectives  181 us (59%)
  waiting for transfers between devices  47.3 us (16%)
  starting transfers between devices  46.1 us (15%)
  matrix products  19.7 us (6%)
  local copies, waits for them, and re-layouts  8.09 us (3%)
    all_to_all x2, blocking collectives, send_back(): lax.all_to_all(routed_in.reshape(crop_count * group_count, local_modes, 1...  50 us
    all_to_all x2, blocking collectives, scatter_x(): whole = lax.all_to_all(whole, 'zh', split_axis=1, concat_axis=2, tiled=True)  47.6 us
    all_to_all x1, blocking collectives, send_out(): lax.all_to_all(ordered, 'dp', split_axis=2, concat_axis=0, tiled=True)  30.1 us
    all_to_all x2, blocking collectives, gather_x(): local = lax.all_to_all(local, 'yc', split_axis=2, concat_axis=1, tiled=True)  29.6 us
    all_to_all x1, blocking collectives, gather_x(): return lax.all_to_all(local, 'zh', split_axis=2, concat_axis=1, tiled=True)  23.7 us
    all_to_all x1, waiting for transfers between devices, gather_x(): return lax.all_to_all(local, 'zh', split_axis=2, concat_axis=1, tiled=True)  21.5 us
    all_to_all x1, waiting for transfers between devices, send_out(): lax.all_to_all(ordered, 'dp', split_axis=2, concat_axis=0, tiled=True)  20.7 us
    dot_general x18, matrix products, bdot(): return jnp.einsum(form, left, right, preferred_element_type=jnp.float32)  19.7 us
  transfers between devices with their start and end apart: 4, of which 4 were waited for; matrix products, arithmetic and copies ran while one was open for 2% of the time, Pallas kernels for 0%

profile of v2, /device:TPU:1, one launch (start us, length us, event | category | flops | bytes accessed | tf_op | source)
XLA Modules:
  0.0 303.8 jit_solution(17345192006387408333)
XLA Ops:
  1.0 0.7 copy-done
  2.9 21.3 %all_to_all.162 = bf16[8,2,2048]{2,1,0:T(2,128)(2,1)S(1)} all-to-all(bf16[8,2,2048]{2,1,0:T(2,128)(2,1)S(1)} %reshape.203), channel_id=1, replica_groups=mesh['zh'=2,'yc'=8,'dp'=64] {'yc'}, dimensions={0} | all-to-all | bytes 131072 | tf_op jit(solution)/shard_map/all_to_all | solution.py:63
  24.4 0.8 reshape.205
  25.2 17.3 %all-to-all-start.1 = ((bf16[2,2,8192]{2,1,0:T(2,128)(2,1)}), bf16[2,2,8192]{2,1,0:T(2,128)(2,1)S(1)}, u32[]{:S(2)}, u32[]{:S(2)}) async-start(bf16[2,2,8192]{2,1,0:T(2,128)(2,1)} %reshape.205), calls=%async_computation.1 | async-start | bytes 131072 | tf_op jit(solution)/shard_map/all_to_all | solution.py:64
  42.7 21.5 %all-to-all-done.1 = bf16[2,2,8192]{2,1,0:T(2,128)(2,1)S(1)} async-done(((bf16[2,2,8192]{2,1,0:T(2,128)(2,1)}), bf16[2,2,8192]{2,1,0:T(2,128)(2,1)S(1)}, u32[]{:S(2)}, u32[]{:S(2)}) %all-to-all-start.1) | async-done | bytes 65568 | tf_op jit(solution)/shard_map/all_to_all | solution.py:64
  65.3 11.8 %all-to-all-start.2 = ((bf16[64,2,128]{2,1,0:T(2,128)(2,1)}), bf16[64,2,128]{2,1,0:T(2,128)(2,1)S(1)}, u32[]{:S(2)}, u32[]{:S(2)}) async-start(bf16[64,2,128]{2,1,0:T(2,128)(2,1)} %reshape.207), calls=%async_computation.2 | async-start | bytes 65536 | tf_op jit(solution)/shard_map/all_to_all | solution.py:87
  77.3 20.7 %all-to-all-done.2 = bf16[64,2,128]{2,1,0:T(2,128)(2,1)S(1)} async-done(((bf16[64,2,128]{2,1,0:T(2,128)(2,1)}), bf16[64,2,128]{2,1,0:T(2,128)(2,1)S(1)}, u32[]{:S(2)}, u32[]{:S(2)}) %all-to-all-start.2) | async-done | bytes 32800 | tf_op jit(solution)/shard_map/all_to_all | solution.py:87
  98.4 25.0 %all_to_all.163 = bf16[64,2,128]{2,1,0:T(2,128)(2,1)S(1)} all-to-all(bf16[64,2,128]{2,1,0:T(2,128)(2,1)S(1)} %reshape.209), channel_id=1, replica_groups=mesh['zh'=2,'yc'=8,'dp'=64] {'dp'}, dimensions={0} | all-to-all | bytes 65536 | tf_op jit(solution)/shard_map/all_to_all | solution.py:91
  123.9 23.9 %all_to_all.164 = bf16[2,2,8192]{2,1,0:T(2,128)(2,1)S(1)} all-to-all(bf16[2,2,8192]{2,1,0:T(2,128)(2,1)S(1)} %reshape.211), channel_id=1, replica_groups=mesh['zh'=2,'yc'=8,'dp'=64] {'zh'}, dimensions={0} | all-to-all | bytes 131072 | tf_op jit(solution)/shard_map/all_to_all | solution.py:67
  148.1 0.8 reshape.213
  148.9 8.9 %all-to-all-start.5 = ((bf16[8,2,2048]{2,1,0:T(2,128)(2,1)}), bf16[8,2,2048]{2,1,0:T(2,128)(2,1)S(1)}, u32[]{:S(2)}, u32[]{:S(2)}) async-start(bf16[8,2,2048]{2,1,0:T(2,128)(2,1)} %reshape.213), calls=%async_computation.5 | async-start | bytes 131072 | tf_op jit(solution)/shard_map/all_to_all | solution.py:68
  157.8 3.7 %fusion.49 = f32[256,2,24,128]{3,0,2,1:T(8,128)} fusion(bf16[1,2,24,64,128]{4,3,2,1,0:T(8,128)(2,1)S(1)} %copy-done, bf16[64,256]{1,0:T(8,128)(2,1)S(1)} %copy-done.1), kind=kOutput, calls=%fused_computation.59 | convolution fusion | flops 201326592 | bytes 7110656 | tf_op jit(solution)/shard_map/bxycz,ch->bxyhz/dot_general | solution.py:43
  161.5 1.2 all-to-all-done.5
  163.5 4.4 %fusion.34 = bf16[2,24,64,128]{3,2,1,0:T(8,128)(2,1)S(1)} fusion(f32[2,24,64,128]{3,2,1,0:T(8,128)S(1)} %fusion.54, f32[256,2,24,128]{3,0,2,1:T(8,128)} %fusion.49, f32[256]{0:T(256)S(1)} %copy-done.5, bf16[1,2,24,64,128]{4,3,2,1,0:T(8,128)(2,1)S(1)} %copy-done.3, f32[64]{0:T(128)S(1)} %copy-done.6, bf16[256,64]{0,1:T(8,128)(2,1)S(1)} %copy-done.4), kind=kOutput, calls=%fused_computation.33 | convolution fusion | flops 216268800 | bytes 9471232 | tf_op jit(solution)/shard_map/bxyhz,hc->bxycz/dot_general | solution.py:43
  169.1 8.3 %all_to_all.165 = bf16[8,2,2048]{2,1,0:T(2,128)(2,1)S(1)} all-to-all(bf16[8,2,2048]{2,1,0:T(2,128)(2,1)S(1)} %reshape.215), channel_id=1, replica_groups=mesh['zh'=2,'yc'=8,'dp'=64] {'yc'}, dimensions={0} | all-to-all | bytes 131072 | tf_op jit(solution)/shard_map/all_to_all | solution.py:63
  177.8 23.7 %all_to_all.166 = bf16[2,2,8192]{2,1,0:T(2,128)(2,1)S(1)} all-to-all(bf16[2,2,8192]{2,1,0:T(2,128)(2,1)S(1)} %reshape.217), channel_id=1, replica_groups=mesh['zh'=2,'yc'=8,'dp'=64] {'zh'}, dimensions={0} | all-to-all | bytes 131072 | tf_op jit(solution)/shard_map/all_to_all | solution.py:64
  201.9 30.1 %all_to_all.167 = bf16[64,2,128]{2,1,0:T(2,128)(2,1)S(1)} all-to-all(bf16[64,2,128]{2,1,0:T(2,128)(2,1)S(1)} %reshape.219), channel_id=1, replica_groups=mesh['zh'=2,'yc'=8,'dp'=64] {'dp'}, dimensions={0} | all-to-all | bytes 65536 | tf_op jit(solution)/shard_map/all_to_all | solution.py:87
  232.4 25.0 %all_to_all.168 = bf16[64,2,128]{2,1,0:T(2,128)(2,1)S(1)} all-to-all(bf16[64,2,128]{2,1,0:T(2,128)(2,1)S(1)} %reshape.221), channel_id=1, replica_groups=mesh['zh'=2,'yc'=8,'dp'=64] {'dp'}, dimensions={0} | all-to-all | bytes 65536 | tf_op jit(solution)/shard_map/all_to_all | solution.py:91
  258.0 23.8 %all_to_all.169 = bf16[2,2,8192]{2,1,0:T(2,128)(2,1)S(1)} all-to-all(bf16[2,2,8192]{2,1,0:T(2,128)(2,1)S(1)} %reshape.223), channel_id=1, replica_groups=mesh['zh'=2,'yc'=8,'dp'=64] {'zh'}, dimensions={0} | all-to-all | bytes 131072 | tf_op jit(solution)/shard_map/all_to_all | solution.py:67
  282.1 0.8 reshape.225
  282.8 8.0 %all-to-all-start.11 = ((bf16[8,2,2048]{2,1,0:T(2,128)(2,1)}), bf16[8,2,2048]{2,1,0:T(2,128)(2,1)S(1)}, u32[]{:S(2)}, u32[]{:S(2)}) async-start(bf16[8,2,2048]{2,1,0:T(2,128)(2,1)} %reshape.225), calls=%async_computation.11 | async-start | bytes 131072 | tf_op jit(solution)/shard_map/all_to_all | solution.py:68
  291.1 0.7 reshape.197
  291.8 3.9 %all-to-all-done.11 = bf16[8,2,2048]{2,1,0:T(2,128)(2,1)S(1)} async-done(((bf16[8,2,2048]{2,1,0:T(2,128)(2,1)}), bf16[8,2,2048]{2,1,0:T(2,128)(2,1)S(1)}, u32[]{:S(2)}, u32[]{:S(2)}) %all-to-all-start.11) | async-done | bytes 65568 | tf_op jit(solution)/shard_map/all_to_all | solution.py:68
  296.5 7.3 %fusion.27 = bf16[1,2,24,64,128]{4,3,2,1,0:T(8,128)(2,1)} fusion(f32[2,24,64,128]{3,2,1,0:T(8,128)S(1)} %fusion.51, f32[256]{0:T(256)S(1)} %copy-done.5, f32[256,2,24,128]{3,0,2,1:T(8,128)} %fusion.49, bf16[2,24,64,128]{3,2,1,0:T(8,128)(2,1)S(1)} %fusion.34, bf16[256,64]{0,1:T(8,128)(2,1)S(1)} %copy-done.4, bf16[64,256]{1,0:T(8,128)(2,1)S(1)} %copy-done.1), kind=kOutput, calls=%fused_computation.29 | convolution fusion | flops 421134336 | bytes 9503744 | tf_op jit(solution)/shard_map/bxyhz,ch->bxycz/dot_general | solution.py:43
  (81 shorter events, 9.1 us)
Async XLA Ops:
  0.6 1.1 copy-start
  0.6 76.5 %copy-start.2 = (bf16[1,4,4096]{2,1,0:T(4,128)(2,1)S(1)}, bf16[1,4,4096]{2,1,0:T(4,128)(2,1)}, u32[]{:S(2)}) copy-start(bf16[1,4,4096]{2,1,0:T(4,128)(2,1)} %param.9) | copy-start | bytes 98308
  2.5 155.3 %copy-start.1 = (bf16[64,256]{1,0:T(8,128)(2,1)S(1)}, bf16[64,256]{1,0:T(8,128)(2,1)}, u32[]{:S(2)}) copy-start(bf16[64,256]{1,0:T(8,128)(2,1)} %param.10) | copy-start | bytes 98308
  25.2 39.0 %all-to-all-start.1 = ((bf16[2,2,8192]{2,1,0:T(2,128)(2,1)}), bf16[2,2,8192]{2,1,0:T(2,128)(2,1)S(1)}, u32[]{:S(2)}, u32[]{:S(2)}) async-start(bf16[2,2,8192]{2,1,0:T(2,128)(2,1)} %reshape.205), calls=%async_computation.1 | async-start | bytes 131072 | tf_op jit(solution)/shard_map/all_to_all | solution.py:64
  65.3 32.7 %all-to-all-start.2 = ((bf16[64,2,128]{2,1,0:T(2,128)(2,1)}), bf16[64,2,128]{2,1,0:T(2,128)(2,1)S(1)}, u32[]{:S(2)}, u32[]{:S(2)}) async-start(bf16[64,2,128]{2,1,0:T(2,128)(2,1)} %reshape.207), calls=%async_computation.2 | async-start | bytes 65536 | tf_op jit(solution)/shard_map/all_to_all | solution.py:87
  148.9 13.8 %all-to-all-start.5 = ((bf16[8,2,2048]{2,1,0:T(2,128)(2,1)}), bf16[8,2,2048]{2,1,0:T(2,128)(2,1)S(1)}, u32[]{:S(2)}, u32[]{:S(2)}) async-start(bf16[8,2,2048]{2,1,0:T(2,128)(2,1)} %reshape.213), calls=%async_computation.5 | async-start | bytes 131072 | tf_op jit(solution)/shard_map/all_to_all | solution.py:68
  157.8 5.7 %copy-start.3 = (bf16[1,2,24,64,128]{4,3,2,1,0:T(8,128)(2,1)S(1)}, bf16[1,2,24,64,128]{4,3,2,1,0:T(8,128)(2,1)}, u32[]{:S(2)}) copy-start(bf16[1,2,24,64,128]{4,3,2,1,0:T(8,128)(2,1)} %param.8) | copy-start | bytes 2359300
  157.8 5.7 %copy-start.4 = (bf16[256,64]{0,1:T(8,128)(2,1)S(1)}, bf16[256,64]{0,1:T(8,128)(2,1)}, u32[]{:S(2)}) copy-start(bf16[256,64]{0,1:T(8,128)(2,1)} %param.12) | copy-start | bytes 98308
  157.8 5.7 %copy-start.5 = (f32[256]{0:T(256)S(1)}, f32[256]{0:T(256)}, u32[]{:S(2)}) copy-start(f32[256]{0:T(256)} %param.11) | copy-start | bytes 3076
  157.8 5.7 %copy-start.6 = (f32[64]{0:T(128)S(1)}, f32[64]{0:T(128)}, u32[]{:S(2)}) copy-start(f32[64]{0:T(128)} %param.13) | copy-start | bytes 772
  282.8 12.9 %all-to-all-start.11 = ((bf16[8,2,2048]{2,1,0:T(2,128)(2,1)}), bf16[8,2,2048]{2,1,0:T(2,128)(2,1)S(1)}, u32[]{:S(2)}, u32[]{:S(2)}) async-start(bf16[8,2,2048]{2,1,0:T(2,128)(2,1)} %reshape.225), calls=%async_computation.11 | async-start | bytes 131072 | tf_op jit(solution)/shard_map/all_to_all | solution.py:68

commit v3 on v2

--- a/solution.py
+++ b/solution.py
@@ -56,52 +56,55 @@
     table_z = dft_table(NZ, MZ)
     factor = 8.0 / (NX * NY * NZ)
 
-    def gather_x(local):
+    def gather_inner(local):
         b_, xl, nj, c_, k_ = local.shape
         local = local.reshape(b_, xl, outer_count, inner_count, c_, k_)
         local = jnp.transpose(local, (0, 1, 3, 2, 4, 5)).reshape(b_, xl, nj, c_, k_)
-        local = lax.all_to_all(local, "yc", split_axis=2, concat_axis=1, tiled=True)
-        return lax.all_to_all(local, "zh", split_axis=2, concat_axis=1, tiled=True)
+        return lax.all_to_all(local, "yc", split_axis=2, concat_axis=1, tiled=True)
 
-    def scatter_x(whole):
-        whole = lax.all_to_all(whole, "zh", split_axis=1, concat_axis=2, tiled=True)
+    def scatter_inner(whole):
         whole = lax.all_to_all(whole, "yc", split_axis=1, concat_axis=2, tiled=True)
         b_, xl, nj, c_, k_ = whole.shape
         whole = whole.reshape(b_, xl, inner_count, outer_count, c_, k_)
         return jnp.transpose(whole, (0, 1, 3, 2, 4, 5)).reshape(b_, xl, nj, c_, k_)
 
+    half_cells = NX // outer_count
+    table_half = lax.dynamic_slice_in_dim(
+        table_x, lax.axis_index("zh") * half_cells, half_cells, axis=1
+    )
+    owners = ("zh", "dp")
+
     def analyse(samples):
         along_z = bdot("bxycz,kz->bxyck", samples, table_z).astype(jnp.bfloat16)
         along_y = bdot("bxyck,jy->bxjck", along_z, table_y).astype(jnp.bfloat16)
-        return bdot("bxjck,ix->bijck", gather_x(along_y), table_x).astype(jnp.bfloat16)
+        partial = bdot("bxjck,ix->jbikc", gather_inner(along_y), table_half)
+        ordered = partial.reshape(outer_count, crop_count, group_count, group_modes, C)
+        ordered = jnp.transpose(ordered, (0, 2, 1, 3, 4)).reshape(
+            outer_count * group_count * crop_count, group_modes, C
+        )
+        arrived = lax.all_to_all(ordered, owners, split_axis=0, concat_axis=0, tiled=True)
+        summed = arrived.reshape(outer_count, group_count * crop_count, group_modes, C).sum(0)
+        return summed.astype(jnp.bfloat16).reshape(
+            group_count * crop_count, local_modes, group_modes, C
+        )
 
-    def synthesise(coeff_in):
-        back_x = bdot("bijck,ix->bxjck", coeff_in, table_x).astype(jnp.bfloat16)
-        back_y = bdot("bxjck,jy->bxyck", scatter_x(back_x), table_y).astype(jnp.bfloat16)
+    def synthesise(routed_in):
+        sent = jnp.broadcast_to(
+            routed_in.reshape(1, group_count * crop_count, group_modes, C),
+            (outer_count, group_count * crop_count, group_modes, C),
+        ).reshape(outer_count * group_count * crop_count, group_modes, C)
+        arrived = lax.all_to_all(sent, owners, split_axis=0, concat_axis=0, tiled=True)
+        arrived = jnp.transpose(
+            arrived.reshape(outer_count, group_count, crop_count, group_modes, C), (2, 0, 1, 3, 4)
+        ).reshape(crop_count, outer_count, MX, MZ, C)
+        back_x = bdot("bjiko,ix->bxjok", arrived, table_half).astype(jnp.bfloat16)
+        back_y = bdot("bxjck,jy->bxyck", scatter_inner(back_x), table_y).astype(jnp.bfloat16)
         return bdot("bxyck,kz->bxycz", back_y, table_z) * factor
 
-    def send_out(coeff_in):
-        ordered = jnp.transpose(coeff_in, (0, 2, 1, 4, 3)).reshape(
-            crop_count, local_modes, group_count, group_modes, C
-        )
-        arrived = lax.all_to_all(ordered, "dp", split_axis=2, concat_axis=0, tiled=True)
-        return arrived.reshape(crop_count * group_count, local_modes, group_modes, C)
-
-    def send_back(routed_in):
-        returned = lax.all_to_all(
-            routed_in.reshape(crop_count * group_count, local_modes, 1, group_modes, C),
-            "dp", split_axis=0, concat_axis=2, tiled=True,
-        )
-        return jnp.transpose(
-            returned.reshape(crop_count, local_modes, MX, MZ, C), (0, 2, 1, 4, 3)
-        )
-
     weights = spectral_weight.reshape(local_modes, group_modes, C, C)
-    coeffs = analyse(inputs)
-    routed = send_out(coeffs)
+    routed = analyse(inputs)
     mixed_routed = bdot("bjgc,jgco->bjgo", routed, weights).astype(jnp.bfloat16)
-    mixed_modes = send_back(mixed_routed)
-    spectral = synthesise(mixed_modes)
+    spectral = synthesise(mixed_routed)
     activation = bdot("bxycz,ch->bxyhz", inputs, w_in) + b_in[:, None]
     hidden = gelu_value(activation).astype(jnp.bfloat16)
     pre_gelu = bdot("bxyhz,hc->bxycz", hidden, w_out) + b_out[:, None] + spectral
@@ -109,14 +112,12 @@
     grad_act = (bdot("bxycz,hc->bxyhz", grad_pre, w_out) * gelu_slope(activation)).astype(
         jnp.bfloat16
     )
-    grad_coeffs = analyse(grad_pre)
-    grad_routed = send_out(grad_coeffs)
+    grad_routed = analyse(grad_pre)
     back_routed = bdot("bjgo,jgco->bjgc", grad_routed, weights).astype(jnp.bfloat16)
-    back_modes = send_back(back_routed)
     grad_weight = (bdot("bjgc,bjgo->jgco", routed, grad_routed) * factor).reshape(
         local_modes, group_modes, C * C
     )
-    grad_field = (bdot("bxyhz,ch->bxycz", grad_act, w_in) + synthesise(back_modes)).astype(
+    grad_field = (bdot("bxyhz,ch->bxycz", grad_act, w_in) + synthesise(back_routed)).astype(
         jnp.bfloat16
     )
     return (grad_field, grad_weight)

time: 305 us -> 230 us (0.75)
  blocking collectives: 181 us -> 106 us
  waiting for transfers between devices: 47.3 us -> 40.1 us
  starting transfers between devices: 46.1 us -> 52 us
    all_to_all x8 -> x4, blocking collectives: 181 us -> 106 us  [the longest x2 61.5 us: synthesise(): lax.all_to_all(sent, owners, split_axis=0, concat_axis=0, tiled=True)]
    all_to_all x4, waiting for transfers between devices: 47.3 us -> 40.1 us  [the longest x1 30.3 us: analyse(): lax.all_to_all(ordered, owners, split_axis=0, concat_axis=0, tiled=True)]
    all_to_all x4, starting transfers between devices: 46.1 us -> 52 us  [the longest x1 21.3 us: analyse(): lax.all_to_all(ordered, owners, split_axis=0, concat_axis=0, tiled=True)]
    unnamed x38 -> x30, local copies, waits for them, and re-layouts: 6.44 us -> 5.73 us
where the time goes in v3:
time: 230 us
  blocking collectives  106 us (46%)
  starting transfers between devices  52 us (23%)
  waiting for transfers between devices  40.1 us (17%)
  matrix products  19.7 us (9%)
  local copies, waits for them, and re-layouts  8.03 us (3%)
  other arithmetic  2.64 us (1%)
    all_to_all x2, blocking collectives, synthesise(): lax.all_to_all(sent, owners, split_axis=0, concat_axis=0, tiled=True)  61.5 us
    all_to_all x1, blocking collectives, analyse(): lax.all_to_all(ordered, owners, split_axis=0, concat_axis=0, tiled=True)  36.4 us
    all_to_all x1, waiting for transfers between devices, analyse(): lax.all_to_all(ordered, owners, split_axis=0, concat_axis=0, tiled=True)  30.3 us
    all_to_all x1, starting transfers between devices, analyse(): lax.all_to_all(ordered, owners, split_axis=0, concat_axis=0, tiled=True)  21.3 us
    dot_general x18, matrix products, bdot(): return jnp.einsum(form, left, right, preferred_element_type=jnp.float32)  19.7 us
    all_to_all x1, starting transfers between devices, gather_inner(): return lax.all_to_all(local, 'yc', split_axis=2, concat_axis=1, tiled=True)  17.4 us
    all_to_all x2, starting transfers between devices, scatter_inner(): whole = lax.all_to_all(whole, 'yc', split_axis=1, concat_axis=2, tiled=True)  13.3 us
    all_to_all x1, blocking collectives, gather_inner(): return lax.all_to_all(local, 'yc', split_axis=2, concat_axis=1, tiled=True)  8.31 us
  transfers between devices with their start and end apart: 4, of which 4 were waited for; matrix products, arithmetic and copies ran while one was open for 2% of the time, Pallas kernels for 0%

profile of v3, /device:TPU:1, one launch (start us, length us, event | category | flops | bytes accessed | tf_op | source)
XLA Modules:
  0.0 229.8 jit_solution(15151820287608750580)
XLA Ops:
  1.0 0.7 copy-done
  2.8 0.8 reshape.173
  3.5 17.4 %all-to-all-start = ((bf16[8,2,2048]{2,1,0:T(2,128)(2,1)}), bf16[8,2,2048]{2,1,0:T(2,128)(2,1)S(1)}, u32[]{:S(2)}, u32[]{:S(2)}) async-start(bf16[8,2,2048]{2,1,0:T(2,128)(2,1)} %reshape.173), calls=%async_computation | async-start | bytes 131072 | tf_op jit(solution)/shard_map/all_to_all | solution.py:63
  21.1 4.6 %all-to-all-done = bf16[8,2,2048]{2,1,0:T(2,128)(2,1)S(1)} async-done(((bf16[8,2,2048]{2,1,0:T(2,128)(2,1)}), bf16[8,2,2048]{2,1,0:T(2,128)(2,1)S(1)}, u32[]{:S(2)}, u32[]{:S(2)}) %all-to-all-start) | async-done | bytes 65568 | tf_op jit(solution)/shard_map/all_to_all | solution.py:63
  26.3 0.9 reshape.175
  27.2 21.3 %all-to-all-start.1 = ((f32[128,1,256]{2,1,0:T(1,128)}), f32[128,1,256]{2,1,0:T(1,128)S(1)}, u32[]{:S(2)}, u32[]{:S(2)}) async-start(f32[128,1,256]{2,1,0:T(1,128)} %reshape.175), calls=%async_computation.1 | async-start | bytes 262144 | tf_op jit(solution)/shard_map/all_to_all | solution.py:85
  48.7 30.3 %all-to-all-done.1 = f32[128,1,256]{2,1,0:T(1,128)S(1)} async-done(((f32[128,1,256]{2,1,0:T(1,128)}), f32[128,1,256]{2,1,0:T(1,128)S(1)}, u32[]{:S(2)}, u32[]{:S(2)}) %all-to-all-start.1) | async-done | bytes 131104 | tf_op jit(solution)/shard_map/all_to_all | solution.py:85
  79.5 1.0 reduce
  81.3 30.8 %all_to_all.74 = bf16[128,2,128]{2,1,0:T(2,128)(2,1)S(1)} all-to-all(bf16[128,2,128]{2,1,0:T(2,128)(2,1)S(1)} %reshape.177), channel_id=1, replica_groups=mesh['zh'=2,'yc'=8,'dp'=64] {'zh','dp'}, dimensions={0} | all-to-all | bytes 131072 | tf_op jit(solution)/shard_map/all_to_all | solution.py:96
  112.5 0.8 reshape.179
  113.3 6.7 %all-to-all-start.3 = ((bf16[8,2,2048]{2,1,0:T(2,128)(2,1)}), bf16[8,2,2048]{2,1,0:T(2,128)(2,1)S(1)}, u32[]{:S(2)}, u32[]{:S(2)}) async-start(bf16[8,2,2048]{2,1,0:T(2,128)(2,1)} %reshape.179), calls=%async_computation.3 | async-start | bytes 131072 | tf_op jit(solution)/shard_map/all_to_all | solution.py:66
  120.0 3.7 %fusion.47 = f32[256,2,24,128]{3,0,2,1:T(8,128)} fusion(bf16[1,2,24,64,128]{4,3,2,1,0:T(8,128)(2,1)S(1)} %copy-done, bf16[64,256]{1,0:T(8,128)(2,1)S(1)} %copy-done.1), kind=kOutput, calls=%fused_computation.57 | convolution fusion | flops 201326592 | bytes 7110656 | tf_op jit(solution)/shard_map/bxycz,ch->bxyhz/dot_general | solution.py:43
  123.6 1.2 all-to-all-done.3
  125.7 4.4 %fusion.34 = bf16[2,24,64,128]{3,2,1,0:T(8,128)(2,1)S(1)} fusion(f32[2,24,64,128]{3,2,1,0:T(8,128)S(1)} %fusion.52, f32[256,2,24,128]{3,0,2,1:T(8,128)} %fusion.47, f32[256]{0:T(256)S(1)} %copy-done.5, bf16[1,2,24,64,128]{4,3,2,1,0:T(8,128)(2,1)S(1)} %copy-done.3, f32[64]{0:T(128)S(1)} %copy-done.6, bf16[256,64]{0,1:T(8,128)(2,1)S(1)} %copy-done.4), kind=kOutput, calls=%fused_computation.33 | convolution fusion | flops 216268800 | bytes 9471232 | tf_op jit(solution)/shard_map/bxyhz,hc->bxycz/dot_general | solution.py:43
  130.1 0.7 convolution_convert_fusion.1
  131.3 8.3 %all_to_all.75 = bf16[8,2,2048]{2,1,0:T(2,128)(2,1)S(1)} all-to-all(bf16[8,2,2048]{2,1,0:T(2,128)(2,1)S(1)} %reshape.181), channel_id=1, replica_groups=mesh['zh'=2,'yc'=8,'dp'=64] {'yc'}, dimensions={0} | all-to-all | bytes 131072 | tf_op jit(solution)/shard_map/all_to_all | solution.py:63
  140.4 36.4 %all_to_all.76 = f32[128,1,256]{2,1,0:T(1,128)S(1)} all-to-all(f32[128,1,256]{2,1,0:T(1,128)S(1)} %reshape.183), channel_id=1, replica_groups=mesh['zh'=2,'yc'=8,'dp'=64] {'zh','dp'}, dimensions={0} | all-to-all | bytes 262144 | tf_op jit(solution)/shard_map/all_to_all | solution.py:85
  176.8 1.0 reduce.1
  178.4 30.6 %all_to_all.77 = bf16[128,2,128]{2,1,0:T(2,128)(2,1)S(1)} all-to-all(bf16[128,2,128]{2,1,0:T(2,128)(2,1)S(1)} %reshape.185), channel_id=1, replica_groups=mesh['zh'=2,'yc'=8,'dp'=64] {'zh','dp'}, dimensions={0} | all-to-all | bytes 131072 | tf_op jit(solution)/shard_map/all_to_all | solution.py:96
  209.4 0.8 reshape.187
  210.2 6.7 %all-to-all-start.7 = ((bf16[8,2,2048]{2,1,0:T(2,128)(2,1)}), bf16[8,2,2048]{2,1,0:T(2,128)(2,1)S(1)}, u32[]{:S(2)}, u32[]{:S(2)}) async-start(bf16[8,2,2048]{2,1,0:T(2,128)(2,1)} %reshape.187), calls=%async_computation.7 | async-start | bytes 131072 | tf_op jit(solution)/shard_map/all_to_all | solution.py:66
  217.0 0.7 reshape.165
  217.7 4.0 %all-to-all-done.7 = bf16[8,2,2048]{2,1,0:T(2,128)(2,1)S(1)} async-done(((bf16[8,2,2048]{2,1,0:T(2,128)(2,1)}), bf16[8,2,2048]{2,1,0:T(2,128)(2,1)S(1)}, u32[]{:S(2)}, u32[]{:S(2)}) %all-to-all-start.7) | async-done | bytes 65568 | tf_op jit(solution)/shard_map/all_to_all | solution.py:66
  222.6 7.3 %fusion.27 = bf16[1,2,24,64,128]{4,3,2,1,0:T(8,128)(2,1)} fusion(f32[2,24,64,128]{3,2,1,0:T(8,128)S(1)} %fusion.49, f32[256]{0:T(256)S(1)} %copy-done.5, f32[256,2,24,128]{3,0,2,1:T(8,128)} %fusion.47, bf16[2,24,64,128]{3,2,1,0:T(8,128)(2,1)S(1)} %fusion.34, bf16[256,64]{0,1:T(8,128)(2,1)S(1)} %copy-done.4, bf16[64,256]{1,0:T(8,128)(2,1)S(1)} %copy-done.1), kind=kOutput, calls=%fused_computation.29 | convolution fusion | flops 421134336 | bytes 9503744 | tf_op jit(solution)/shard_map/bxyhz,ch->bxycz/dot_general | solution.py:43
  (70 shorter events, 7.7 us)
Async XLA Ops:
  0.6 1.1 copy-start
  0.6 47.9 %copy-start.2 = (bf16[1,4,4096]{2,1,0:T(4,128)(2,1)S(1)}, bf16[1,4,4096]{2,1,0:T(4,128)(2,1)}, u32[]{:S(2)}) copy-start(bf16[1,4,4096]{2,1,0:T(4,128)(2,1)} %param.9) | copy-start | bytes 98308
  2.7 117.3 %copy-start.1 = (bf16[64,256]{1,0:T(8,128)(2,1)S(1)}, bf16[64,256]{1,0:T(8,128)(2,1)}, u32[]{:S(2)}) copy-start(bf16[64,256]{1,0:T(8,128)(2,1)} %param.10) | copy-start | bytes 98308
  3.5 22.2 %all-to-all-start = ((bf16[8,2,2048]{2,1,0:T(2,128)(2,1)}), bf16[8,2,2048]{2,1,0:T(2,128)(2,1)S(1)}, u32[]{:S(2)}, u32[]{:S(2)}) async-start(bf16[8,2,2048]{2,1,0:T(2,128)(2,1)} %reshape.173), calls=%async_computation | async-start | bytes 131072 | tf_op jit(solution)/shard_map/all_to_all | solution.py:63
  27.2 51.8 %all-to-all-start.1 = ((f32[128,1,256]{2,1,0:T(1,128)}), f32[128,1,256]{2,1,0:T(1,128)S(1)}, u32[]{:S(2)}, u32[]{:S(2)}) async-start(f32[128,1,256]{2,1,0:T(1,128)} %reshape.175), calls=%async_computation.1 | async-start | bytes 262144 | tf_op jit(solution)/shard_map/all_to_all | solution.py:85
  113.3 11.5 %all-to-all-start.3 = ((bf16[8,2,2048]{2,1,0:T(2,128)(2,1)}), bf16[8,2,2048]{2,1,0:T(2,128)(2,1)S(1)}, u32[]{:S(2)}, u32[]{:S(2)}) async-start(bf16[8,2,2048]{2,1,0:T(2,128)(2,1)} %reshape.179), calls=%async_computation.3 | async-start | bytes 131072 | tf_op jit(solution)/shard_map/all_to_all | solution.py:66
  119.9 5.7 %copy-start.3 = (bf16[1,2,24,64,128]{4,3,2,1,0:T(8,128)(2,1)S(1)}, bf16[1,2,24,64,128]{4,3,2,1,0:T(8,128)(2,1)}, u32[]{:S(2)}) copy-start(bf16[1,2,24,64,128]{4,3,2,1,0:T(8,128)(2,1)} %param.8) | copy-start | bytes 2359300
  119.9 5.7 %copy-start.4 = (bf16[256,64]{0,1:T(8,128)(2,1)S(1)}, bf16[256,64]{0,1:T(8,128)(2,1)}, u32[]{:S(2)}) copy-start(bf16[256,64]{0,1:T(8,128)(2,1)} %param.12) | copy-start | bytes 98308
  120.0 5.7 %copy-start.5 = (f32[256]{0:T(256)S(1)}, f32[256]{0:T(256)}, u32[]{:S(2)}) copy-start(f32[256]{0:T(256)} %param.11) | copy-start | bytes 3076
  120.0 5.7 %copy-start.6 = (f32[64]{0:T(128)S(1)}, f32[64]{0:T(128)}, u32[]{:S(2)}) copy-start(f32[64]{0:T(128)} %param.13) | copy-start | bytes 772
  210.2 11.5 %all-to-all-start.7 = ((bf16[8,2,2048]{2,1,0:T(2,128)(2,1)}), bf16[8,2,2048]{2,1,0:T(2,128)(2,1)S(1)}, u32[]{:S(2)}, u32[]{:S(2)}) async-start(bf16[8,2,2048]{2,1,0:T(2,128)(2,1)} %reshape.187), calls=%async_computation.7 | async-start | bytes 131072 | tf_op jit(solution)/shard_map/all_to_all | solution.py:66

commit v4 on v3

--- a/solution.py
+++ b/solution.py
@@ -81,9 +81,11 @@
         ordered = partial.reshape(outer_count, crop_count, group_count, group_modes, C)
         ordered = jnp.transpose(ordered, (0, 2, 1, 3, 4)).reshape(
             outer_count * group_count * crop_count, group_modes, C
-        )
+        ).astype(jnp.bfloat16)
         arrived = lax.all_to_all(ordered, owners, split_axis=0, concat_axis=0, tiled=True)
-        summed = arrived.reshape(outer_count, group_count * crop_count, group_modes, C).sum(0)
+        summed = arrived.astype(jnp.float32).reshape(
+            outer_count, group_count * crop_count, group_modes, C
+        ).sum(0)
         return summed.astype(jnp.bfloat16).reshape(
             group_count * crop_count, local_modes, group_modes, C
         )

time: 230 us -> 217 us (0.943)
  waiting for transfers between devices: 40.1 us -> 34.4 us
  blocking collectives: 106 us -> 102 us
    all_to_all x1, waiting for transfers between devices: 30.3 us -> 24.6 us  [analyse(): lax.all_to_all(ordered, owners, split_axis=0, concat_axis=0, tiled=True)]
    all_to_all x1, blocking collectives: 36.4 us -> 31 us  [analyse(): lax.all_to_all(ordered, owners, split_axis=0, concat_axis=0, tiled=True)]
where the time goes in v4:
time: 217 us
  blocking collectives  102 us (47%)
  starting transfers between devices  52.1 us (24%)
  waiting for transfers between devices  34.4 us (16%)
  matrix products  19.7 us (9%)
  local copies, waits for them, and re-layouts  7.03 us (3%)
    all_to_all x2, blocking collectives, synthesise(): lax.all_to_all(sent, owners, split_axis=0, concat_axis=0, tiled=True)  62.2 us
    all_to_all x1, blocking collectives, analyse(): lax.all_to_all(ordered, owners, split_axis=0, concat_axis=0, tiled=True)  31 us
    all_to_all x1, waiting for transfers between devices, analyse(): lax.all_to_all(ordered, owners, split_axis=0, concat_axis=0, tiled=True)  24.6 us
    all_to_all x1, starting transfers between devices, analyse(): lax.all_to_all(ordered, owners, split_axis=0, concat_axis=0, tiled=True)  21.3 us
    dot_general x18, matrix products, bdot(): return jnp.einsum(form, left, right, preferred_element_type=jnp.float32)  19.7 us
    all_to_all x1, starting transfers between devices, gather_inner(): return lax.all_to_all(local, 'yc', split_axis=2, concat_axis=1, tiled=True)  17.4 us
    all_to_all x2, starting transfers between devices, scatter_inner(): whole = lax.all_to_all(whole, 'yc', split_axis=1, concat_axis=2, tiled=True)  13.4 us
    all_to_all x1, blocking collectives, gather_inner(): return lax.all_to_all(local, 'yc', split_axis=2, concat_axis=1, tiled=True)  8.29 us
  transfers between devices with their start and end apart: 4, of which 4 were waited for; matrix products, arithmetic and copies ran while one was open for 2% of the time, Pallas kernels for 0%

profile of v4, /device:TPU:1, one launch (start us, length us, event | category | flops | bytes accessed | tf_op | source)
XLA Modules:
  0.0 216.7 jit_solution(14787966372436941330)
XLA Ops:
  1.0 0.7 copy-done
  1.8 0.7 fusion.37
  2.7 0.8 reshape.185
  3.5 17.4 %all-to-all-start = ((bf16[8,2,2048]{2,1,0:T(2,128)(2,1)}), bf16[8,2,2048]{2,1,0:T(2,128)(2,1)S(1)}, u32[]{:S(2)}, u32[]{:S(2)}) async-start(bf16[8,2,2048]{2,1,0:T(2,128)(2,1)} %reshape.185), calls=%async_computation | async-start | bytes 131072 | tf_op jit(solution)/shard_map/all_to_all | solution.py:63
  21.1 4.6 %all-to-all-done = bf16[8,2,2048]{2,1,0:T(2,128)(2,1)S(1)} async-done(((bf16[8,2,2048]{2,1,0:T(2,128)(2,1)}), bf16[8,2,2048]{2,1,0:T(2,128)(2,1)S(1)}, u32[]{:S(2)}, u32[]{:S(2)}) %all-to-all-start) | async-done | bytes 65568 | tf_op jit(solution)/shard_map/all_to_all | solution.py:63
  26.3 0.7 reshape.187
  27.0 21.3 %all-to-all-start.1 = ((bf16[128,2,128]{2,1,0:T(2,128)(2,1)}), bf16[128,2,128]{2,1,0:T(2,128)(2,1)S(1)}, u32[]{:S(2)}, u32[]{:S(2)}) async-start(bf16[128,2,128]{2,1,0:T(2,128)(2,1)} %reshape.187), calls=%async_computation.1 | async-start | bytes 131072 | tf_op jit(solution)/shard_map/all_to_all | solution.py:85
  48.5 24.6 %all-to-all-done.1 = bf16[128,2,128]{2,1,0:T(2,128)(2,1)S(1)} async-done(((bf16[128,2,128]{2,1,0:T(2,128)(2,1)}), bf16[128,2,128]{2,1,0:T(2,128)(2,1)S(1)}, u32[]{:S(2)}, u32[]{:S(2)}) %all-to-all-start.1) | async-done | bytes 65568 | tf_op jit(solution)/shard_map/all_to_all | solution.py:85
  73.9 31.4 %all_to_all.74 = bf16[128,2,128]{2,1,0:T(2,128)(2,1)S(1)} all-to-all(bf16[128,2,128]{2,1,0:T(2,128)(2,1)S(1)} %reshape.189), channel_id=1, replica_groups=mesh['zh'=2,'yc'=8,'dp'=64] {'zh','dp'}, dimensions={0} | all-to-all | bytes 131072 | tf_op jit(solution)/shard_map/all_to_all | solution.py:98
  105.6 0.8 reshape.191
  106.4 6.7 %all-to-all-start.3 = ((bf16[8,2,2048]{2,1,0:T(2,128)(2,1)}), bf16[8,2,2048]{2,1,0:T(2,128)(2,1)S(1)}, u32[]{:S(2)}, u32[]{:S(2)}) async-start(bf16[8,2,2048]{2,1,0:T(2,128)(2,1)} %reshape.191), calls=%async_computation.3 | async-start | bytes 131072 | tf_op jit(solution)/shard_map/all_to_all | solution.py:66
  113.1 3.7 %fusion.49 = f32[256,2,24,128]{3,0,2,1:T(8,128)} fusion(bf16[1,2,24,64,128]{4,3,2,1,0:T(8,128)(2,1)S(1)} %copy-done, bf16[64,256]{1,0:T(8,128)(2,1)S(1)} %copy-done.1), kind=kOutput, calls=%fused_computation.59 | convolution fusion | flops 201326592 | bytes 7110656 | tf_op jit(solution)/shard_map/bxycz,ch->bxyhz/dot_general | solution.py:43
  116.8 1.2 all-to-all-done.3
  118.3 0.4 fusion.54
  118.8 4.4 %fusion.34 = bf16[2,24,64,128]{3,2,1,0:T(8,128)(2,1)S(1)} fusion(f32[2,24,64,128]{3,2,1,0:T(8,128)S(1)} %fusion.54, f32[256,2,24,128]{3,0,2,1:T(8,128)} %fusion.49, f32[256]{0:T(256)S(1)} %copy-done.5, bf16[1,2,24,64,128]{4,3,2,1,0:T(8,128)(2,1)S(1)} %copy-done.3, f32[64]{0:T(128)S(1)} %copy-done.6, bf16[256,64]{0,1:T(8,128)(2,1)S(1)} %copy-done.4), kind=kOutput, calls=%fused_computation.33 | convolution fusion | flops 216268800 | bytes 9471232 | tf_op jit(solution)/shard_map/bxyhz,hc->bxycz/dot_general | solution.py:43
  123.2 0.7 convolution_convert_fusion.1
  124.4 8.3 %all_to_all.75 = bf16[8,2,2048]{2,1,0:T(2,128)(2,1)S(1)} all-to-all(bf16[8,2,2048]{2,1,0:T(2,128)(2,1)S(1)} %reshape.193), channel_id=1, replica_groups=mesh['zh'=2,'yc'=8,'dp'=64] {'yc'}, dimensions={0} | all-to-all | bytes 131072 | tf_op jit(solution)/shard_map/all_to_all | solution.py:63
  133.3 31.0 %all_to_all.76 = bf16[128,2,128]{2,1,0:T(2,128)(2,1)S(1)} all-to-all(bf16[128,2,128]{2,1,0:T(2,128)(2,1)S(1)} %reshape.195), channel_id=1, replica_groups=mesh['zh'=2,'yc'=8,'dp'=64] {'zh','dp'}, dimensions={0} | all-to-all | bytes 131072 | tf_op jit(solution)/shard_map/all_to_all | solution.py:85
  164.9 30.9 %all_to_all.77 = bf16[128,2,128]{2,1,0:T(2,128)(2,1)S(1)} all-to-all(bf16[128,2,128]{2,1,0:T(2,128)(2,1)S(1)} %reshape.197), channel_id=1, replica_groups=mesh['zh'=2,'yc'=8,'dp'=64] {'zh','dp'}, dimensions={0} | all-to-all | bytes 131072 | tf_op jit(solution)/shard_map/all_to_all | solution.py:98
  196.2 0.8 reshape.199
  197.0 6.7 %all-to-all-start.7 = ((bf16[8,2,2048]{2,1,0:T(2,128)(2,1)}), bf16[8,2,2048]{2,1,0:T(2,128)(2,1)S(1)}, u32[]{:S(2)}, u32[]{:S(2)}) async-start(bf16[8,2,2048]{2,1,0:T(2,128)(2,1)} %reshape.199), calls=%async_computation.7 | async-start | bytes 131072 | tf_op jit(solution)/shard_map/all_to_all | solution.py:66
  203.8 0.7 reshape.177
  204.6 4.0 %all-to-all-done.7 = bf16[8,2,2048]{2,1,0:T(2,128)(2,1)S(1)} async-done(((bf16[8,2,2048]{2,1,0:T(2,128)(2,1)}), bf16[8,2,2048]{2,1,0:T(2,128)(2,1)S(1)}, u32[]{:S(2)}, u32[]{:S(2)}) %all-to-all-start.7) | async-done | bytes 65568 | tf_op jit(solution)/shard_map/all_to_all | solution.py:66
  209.4 7.3 %fusion.27 = bf16[1,2,24,64,128]{4,3,2,1,0:T(8,128)(2,1)} fusion(f32[2,24,64,128]{3,2,1,0:T(8,128)S(1)} %fusion.51, f32[256]{0:T(256)S(1)} %copy-done.5, f32[256,2,24,128]{3,0,2,1:T(8,128)} %fusion.49, bf16[2,24,64,128]{3,2,1,0:T(8,128)(2,1)S(1)} %fusion.34, bf16[256,64]{0,1:T(8,128)(2,1)S(1)} %copy-done.4, bf16[64,256]{1,0:T(8,128)(2,1)S(1)} %copy-done.1), kind=kOutput, calls=%fused_computation.29 | convolution fusion | flops 421134336 | bytes 9503744 | tf_op jit(solution)/shard_map/bxyhz,ch->bxycz/dot_general | solution.py:43
  (67 shorter events, 5.7 us)
Async XLA Ops:
  0.6 1.1 copy-start
  0.6 47.7 %copy-start.2 = (bf16[1,4,4096]{2,1,0:T(4,128)(2,1)S(1)}, bf16[1,4,4096]{2,1,0:T(4,128)(2,1)}, u32[]{:S(2)}) copy-start(bf16[1,4,4096]{2,1,0:T(4,128)(2,1)} %param.9) | copy-start | bytes 98308
  1.8 111.3 %copy-start.1 = (bf16[64,256]{1,0:T(8,128)(2,1)S(1)}, bf16[64,256]{1,0:T(8,128)(2,1)}, u32[]{:S(2)}) copy-start(bf16[64,256]{1,0:T(8,128)(2,1)} %param.10) | copy-start | bytes 98308
  3.5 22.2 %all-to-all-start = ((bf16[8,2,2048]{2,1,0:T(2,128)(2,1)}), bf16[8,2,2048]{2,1,0:T(2,128)(2,1)S(1)}, u32[]{:S(2)}, u32[]{:S(2)}) async-start(bf16[8,2,2048]{2,1,0:T(2,128)(2,1)} %reshape.185), calls=%async_computation | async-start | bytes 131072 | tf_op jit(solution)/shard_map/all_to_all | solution.py:63
  27.0 46.1 %all-to-all-start.1 = ((bf16[128,2,128]{2,1,0:T(2,128)(2,1)}), bf16[128,2,128]{2,1,0:T(2,128)(2,1)S(1)}, u32[]{:S(2)}, u32[]{:S(2)}) async-start(bf16[128,2,128]{2,1,0:T(2,128)(2,1)} %reshape.187), calls=%async_computation.1 | async-start | bytes 131072 | tf_op jit(solution)/shard_map/all_to_all | solution.py:85
  106.4 11.5 %all-to-all-start.3 = ((bf16[8,2,2048]{2,1,0:T(2,128)(2,1)}), bf16[8,2,2048]{2,1,0:T(2,128)(2,1)S(1)}, u32[]{:S(2)}, u32[]{:S(2)}) async-start(bf16[8,2,2048]{2,1,0:T(2,128)(2,1)} %reshape.191), calls=%async_computation.3 | async-start | bytes 131072 | tf_op jit(solution)/shard_map/all_to_all | solution.py:66
  113.1 5.7 %copy-start.3 = (bf16[1,2,24,64,128]{4,3,2,1,0:T(8,128)(2,1)S(1)}, bf16[1,2,24,64,128]{4,3,2,1,0:T(8,128)(2,1)}, u32[]{:S(2)}) copy-start(bf16[1,2,24,64,128]{4,3,2,1,0:T(8,128)(2,1)} %param.8) | copy-start | bytes 2359300
  113.1 5.7 %copy-start.4 = (bf16[256,64]{0,1:T(8,128)(2,1)S(1)}, bf16[256,64]{0,1:T(8,128)(2,1)}, u32[]{:S(2)}) copy-start(bf16[256,64]{0,1:T(8,128)(2,1)} %param.12) | copy-start | bytes 98308
  113.1 5.7 %copy-start.5 = (f32[256]{0:T(256)S(1)}, f32[256]{0:T(256)}, u32[]{:S(2)}) copy-start(f32[256]{0:T(256)} %param.11) | copy-start | bytes 3076
  113.1 5.7 %copy-start.6 = (f32[64]{0:T(128)S(1)}, f32[64]{0:T(128)}, u32[]{:S(2)}) copy-start(f32[64]{0:T(128)} %param.13) | copy-start | bytes 772
  197.0 11.6 %all-to-all-start.7 = ((bf16[8,2,2048]{2,1,0:T(2,128)(2,1)}), bf16[8,2,2048]{2,1,0:T(2,128)(2,1)S(1)}, u32[]{:S(2)}, u32[]{:S(2)}) async-start(bf16[8,2,2048]{2,1,0:T(2,128)(2,1)} %reshape.199), calls=%async_computation.7 | async-start | bytes 131072 | tf_op jit(solution)/shard_map/all_to_all | solution.py:66

commit v5 on v4

--- a/solution.py
+++ b/solution.py
@@ -109,7 +109,10 @@
     spectral = synthesise(mixed_routed)
     activation = bdot("bxycz,ch->bxyhz", inputs, w_in) + b_in[:, None]
     hidden = gelu_value(activation).astype(jnp.bfloat16)
-    pre_gelu = bdot("bxyhz,hc->bxycz", hidden, w_out) + b_out[:, None] + spectral
+    channel_out, activation = lax.optimization_barrier(
+        (bdot("bxyhz,hc->bxycz", hidden, w_out) + b_out[:, None], activation)
+    )
+    pre_gelu = channel_out + spectral
     grad_pre = (cotangent.astype(jnp.float32) * gelu_slope(pre_gelu)).astype(jnp.bfloat16)
     grad_act = (bdot("bxycz,hc->bxyhz", grad_pre, w_out) * gelu_slope(activation)).astype(
         jnp.bfloat16

time: 217 us -> 216 us (level)
  blocking collectives: 102 us -> 71.1 us
  waiting for transfers between devices: 34.4 us -> 54.3 us
  starting transfers between devices: 52.1 us -> 59 us
    all_to_all x2 -> x1, blocking collectives: 62.2 us -> 30.9 us  [synthesise(): lax.all_to_all(sent, owners, split_axis=0, concat_axis=0, tiled=True)]
    all_to_all x0 -> x1, waiting for transfers between devices: none -> 20.7 us  [synthesise(): lax.all_to_all(sent, owners, split_axis=0, concat_axis=0, tiled=True)]
    all_to_all x0 -> x1, starting transfers between devices: none -> 6.95 us  [synthesise(): lax.all_to_all(sent, owners, split_axis=0, concat_axis=0, tiled=True)]
  transfers between devices with their start and end apart: 4 -> 5, of which waited for: 4 -> 5; matrix products, arithmetic and copies ran while one was open for 2% -> 4% of each run, Pallas kernels for 0% -> 0%
where the time goes in v5:
time: 216 us
  blocking collectives  71.1 us (33%)
  starting transfers between devices  59 us (27%)
  waiting for transfers between devices  54.3 us (25%)
  matrix products  21.7 us (10%)
  local copies, waits for them, and re-layouts  7.66 us (4%)
    all_to_all x1, blocking collectives, analyse(): lax.all_to_all(ordered, owners, split_axis=0, concat_axis=0, tiled=True)  31 us
    all_to_all x1, blocking collectives, synthesise(): lax.all_to_all(sent, owners, split_axis=0, concat_axis=0, tiled=True)  30.9 us
    all_to_all x1, waiting for transfers between devices, analyse(): lax.all_to_all(ordered, owners, split_axis=0, concat_axis=0, tiled=True)  24.7 us
    dot_general x18, matrix products, bdot(): return jnp.einsum(form, left, right, preferred_element_type=jnp.float32)  21.7 us
    all_to_all x1, starting transfers between devices, analyse(): lax.all_to_all(ordered, owners, split_axis=0, concat_axis=0, tiled=True)  21.3 us
    all_to_all x1, waiting for transfers between devices, synthesise(): lax.all_to_all(sent, owners, split_axis=0, concat_axis=0, tiled=True)  20.7 us
    all_to_all x1, starting transfers between devices, gather_inner(): return lax.all_to_all(local, 'yc', split_axis=2, concat_axis=1, tiled=True)  17.4 us
    all_to_all x2, starting transfers between devices, scatter_inner(): whole = lax.all_to_all(whole, 'yc', split_axis=1, concat_axis=2, tiled=True)  13.4 us
  transfers between devices with their start and end apart: 5, of which 5 were waited for; matrix products, arithmetic and copies ran while one was open for 4% of the time, Pallas kernels for 0%

profile of v5, /device:TPU:1, one launch (start us, length us, event | category | flops | bytes accessed | tf_op | source)
XLA Modules:
  0.0 215.7 jit_solution(2268198352852710298)
XLA Ops:
  1.1 0.7 copy-done
  2.7 0.8 reshape.185
  3.5 17.4 %all-to-all-start = ((bf16[8,2,2048]{2,1,0:T(2,128)(2,1)}), bf16[8,2,2048]{2,1,0:T(2,128)(2,1)S(1)}, u32[]{:S(2)}, u32[]{:S(2)}) async-start(bf16[8,2,2048]{2,1,0:T(2,128)(2,1)} %reshape.185), calls=%async_computation | async-start | bytes 131072 | tf_op jit(solution)/shard_map/all_to_all | solution.py:63
  21.1 4.6 %all-to-all-done = bf16[8,2,2048]{2,1,0:T(2,128)(2,1)S(1)} async-done(((bf16[8,2,2048]{2,1,0:T(2,128)(2,1)}), bf16[8,2,2048]{2,1,0:T(2,128)(2,1)S(1)}, u32[]{:S(2)}, u32[]{:S(2)}) %all-to-all-start) | async-done | bytes 65568 | tf_op jit(solution)/shard_map/all_to_all | solution.py:63
  26.3 0.7 reshape.187
  27.0 21.3 %all-to-all-start.1 = ((bf16[128,2,128]{2,1,0:T(2,128)(2,1)}), bf16[128,2,128]{2,1,0:T(2,128)(2,1)S(1)}, u32[]{:S(2)}, u32[]{:S(2)}) async-start(bf16[128,2,128]{2,1,0:T(2,128)(2,1)} %reshape.187), calls=%async_computation.1 | async-start | bytes 131072 | tf_op jit(solution)/shard_map/all_to_all | solution.py:85
  48.5 24.7 %all-to-all-done.1 = bf16[128,2,128]{2,1,0:T(2,128)(2,1)S(1)} async-done(((bf16[128,2,128]{2,1,0:T(2,128)(2,1)}), bf16[128,2,128]{2,1,0:T(2,128)(2,1)S(1)}, u32[]{:S(2)}, u32[]{:S(2)}) %all-to-all-start.1) | async-done | bytes 65568 | tf_op jit(solution)/shard_map/all_to_all | solution.py:85
  73.9 0.7 reshape.189
  74.6 7.0 %all-to-all-start.2 = ((bf16[128,2,128]{2,1,0:T(2,128)(2,1)}), bf16[128,2,128]{2,1,0:T(2,128)(2,1)S(1)}, u32[]{:S(2)}, u32[]{:S(2)}) async-start(bf16[128,2,128]{2,1,0:T(2,128)(2,1)} %reshape.189), calls=%async_computation.2 | async-start | bytes 131072 | tf_op jit(solution)/shard_map/all_to_all | solution.py:98
  81.6 3.6 %fusion.6 = f32[1,2,24,256,128]{4,3,2,1,0:T(8,128)} fusion(f32[256]{0:T(256)S(1)} %copy-done.3, bf16[1,2,24,64,128]{4,3,2,1,0:T(8,128)(2,1)S(1)} %copy-done, bf16[64,256]{1,0:T(8,128)(2,1)S(1)} %copy-done.1), kind=kOutput, calls=%fused_computation.8 | convolution fusion | flops 202899456 | bytes 7111680 | tf_op jit(solution)/shard_map/bxycz,ch->bxyhz/dot_general | solution.py:43
  85.3 20.7 %all-to-all-done.2 = bf16[128,2,128]{2,1,0:T(2,128)(2,1)S(1)} async-done(((bf16[128,2,128]{2,1,0:T(2,128)(2,1)}), bf16[128,2,128]{2,1,0:T(2,128)(2,1)S(1)}, u32[]{:S(2)}, u32[]{:S(2)}) %all-to-all-start.2) | async-done | bytes 65568 | tf_op jit(solution)/shard_map/all_to_all | solution.py:98
  106.4 0.8 reshape.191
  107.2 6.7 %all-to-all-start.3 = ((bf16[8,2,2048]{2,1,0:T(2,128)(2,1)}), bf16[8,2,2048]{2,1,0:T(2,128)(2,1)S(1)}, u32[]{:S(2)}, u32[]{:S(2)}) async-start(bf16[8,2,2048]{2,1,0:T(2,128)(2,1)} %reshape.191), calls=%async_computation.3 | async-start | bytes 131072 | tf_op jit(solution)/shard_map/all_to_all | solution.py:66
  113.9 4.6 %fusion.21 = f32[1,2,24,64,128]{4,3,2,1,0:T(8,128)} fusion(f32[1,2,24,256,128]{4,3,2,1,0:T(8,128)} %fusion.6, f32[64]{0:T(128)S(1)} %copy-done.6, bf16[256,64]{0,1:T(8,128)(2,1)S(1)} %copy-done.5), kind=kOutput, calls=%fused_computation.25 | convolution fusion | flops 209584128 | bytes 7897344 | tf_op jit(solution)/shard_map/bxyhz,hc->bxycz/dot_general | solution.py:43
  119.1 2.5 %fusion.26 = bf16[2,24,64,128]{3,2,1,0:T(8,128)(2,1)S(1)} fusion(f32[1,2,24,64,128]{4,3,2,1,0:T(8,128)} %fusion.21, bf16[1,2,24,64,128]{4,3,2,1,0:T(8,128)(2,1)S(1)} %copy-done.4, bf16[2,24,64,16]{2,1,3,0:T(8,128)(2,1)S(1)} %fusion.28, bf16[8,128]{1,0:T(8,128)(2,1)S(1)} %get-tuple-element.9, bf16[8,128]{1,0:T(8,128)(2,1)S(1)} %get-tuple-element.8), kind=kOutput, calls=%fused_computation.27 | convolution fusion | flops 17702912 | bytes 3248128 | tf_op jit(solution)/shard_map/bxyck,kz->bxycz/dot_general | solution.py:43
  121.6 0.7 convolution_convert_fusion.1
  122.7 9.2 %all_to_all.74 = bf16[8,2,2048]{2,1,0:T(2,128)(2,1)S(1)} all-to-all(bf16[8,2,2048]{2,1,0:T(2,128)(2,1)S(1)} %reshape.193), channel_id=1, replica_groups=mesh['zh'=2,'yc'=8,'dp'=64] {'yc'}, dimensions={0} | all-to-all | bytes 131072 | tf_op jit(solution)/shard_map/all_to_all | solution.py:63
  132.6 31.0 %all_to_all.75 = bf16[128,2,128]{2,1,0:T(2,128)(2,1)S(1)} all-to-all(bf16[128,2,128]{2,1,0:T(2,128)(2,1)S(1)} %reshape.195), channel_id=1, replica_groups=mesh['zh'=2,'yc'=8,'dp'=64] {'zh','dp'}, dimensions={0} | all-to-all | bytes 131072 | tf_op jit(solution)/shard_map/all_to_all | solution.py:85
  164.2 30.9 %all_to_all.76 = bf16[128,2,128]{2,1,0:T(2,128)(2,1)S(1)} all-to-all(bf16[128,2,128]{2,1,0:T(2,128)(2,1)S(1)} %reshape.197), channel_id=1, replica_groups=mesh['zh'=2,'yc'=8,'dp'=64] {'zh','dp'}, dimensions={0} | all-to-all | bytes 131072 | tf_op jit(solution)/shard_map/all_to_all | solution.py:98
  195.5 0.8 reshape.199
  196.3 6.7 %all-to-all-start.7 = ((bf16[8,2,2048]{2,1,0:T(2,128)(2,1)}), bf16[8,2,2048]{2,1,0:T(2,128)(2,1)S(1)}, u32[]{:S(2)}, u32[]{:S(2)}) async-start(bf16[8,2,2048]{2,1,0:T(2,128)(2,1)} %reshape.199), calls=%async_computation.7 | async-start | bytes 131072 | tf_op jit(solution)/shard_map/all_to_all | solution.py:66
  203.1 0.7 reshape.177
  203.8 4.0 %all-to-all-done.7 = bf16[8,2,2048]{2,1,0:T(2,128)(2,1)S(1)} async-done(((bf16[8,2,2048]{2,1,0:T(2,128)(2,1)}), bf16[8,2,2048]{2,1,0:T(2,128)(2,1)S(1)}, u32[]{:S(2)}, u32[]{:S(2)}) %all-to-all-start.7) | async-done | bytes 65568 | tf_op jit(solution)/shard_map/all_to_all | solution.py:66
  208.6 7.1 %fusion.20 = bf16[1,2,24,64,128]{4,3,2,1,0:T(8,128)(2,1)} fusion(f32[2,24,64,128]{3,2,1,0:T(8,128)S(1)} %fusion.40, f32[1,2,24,256,128]{4,3,2,1,0:T(8,128)} %fusion.6, bf16[2,24,64,128]{3,2,1,0:T(8,128)(2,1)S(1)} %fusion.26, bf16[256,64]{0,1:T(8,128)(2,1)S(1)} %copy-done.5, bf16[64,256]{1,0:T(8,128)(2,1)S(1)} %copy-done.1), kind=kOutput, calls=%fused_computation.23 | convolution fusion | flops 419561472 | bytes 9502720 | tf_op jit(solution)/shard_map/bxyhz,ch->bxycz/dot_general | solution.py:43
  (68 shorter events, 6.6 us)
Async XLA Ops:
  0.6 1.1 copy-start
  0.6 47.7 %copy-start.2 = (bf16[1,4,4096]{2,1,0:T(4,128)(2,1)S(1)}, bf16[1,4,4096]{2,1,0:T(4,128)(2,1)}, u32[]{:S(2)}) copy-start(bf16[1,4,4096]{2,1,0:T(4,128)(2,1)} %param.9) | copy-start | bytes 98308
  0.7 81.0 %copy-start.1 = (bf16[64,256]{1,0:T(8,128)(2,1)S(1)}, bf16[64,256]{1,0:T(8,128)(2,1)}, u32[]{:S(2)}) copy-start(bf16[64,256]{1,0:T(8,128)(2,1)} %param.10) | copy-start | bytes 98308
  0.7 81.0 %copy-start.3 = (f32[256]{0:T(256)S(1)}, f32[256]{0:T(256)}, u32[]{:S(2)}) copy-start(f32[256]{0:T(256)} %param.11) | copy-start | bytes 3076
  3.5 22.2 %all-to-all-start = ((bf16[8,2,2048]{2,1,0:T(2,128)(2,1)}), bf16[8,2,2048]{2,1,0:T(2,128)(2,1)S(1)}, u32[]{:S(2)}, u32[]{:S(2)}) async-start(bf16[8,2,2048]{2,1,0:T(2,128)(2,1)} %reshape.185), calls=%async_computation | async-start | bytes 131072 | tf_op jit(solution)/shard_map/all_to_all | solution.py:63
  27.0 46.2 %all-to-all-start.1 = ((bf16[128,2,128]{2,1,0:T(2,128)(2,1)}), bf16[128,2,128]{2,1,0:T(2,128)(2,1)S(1)}, u32[]{:S(2)}, u32[]{:S(2)}) async-start(bf16[128,2,128]{2,1,0:T(2,128)(2,1)} %reshape.187), calls=%async_computation.1 | async-start | bytes 131072 | tf_op jit(solution)/shard_map/all_to_all | solution.py:85
  74.6 31.4 %all-to-all-start.2 = ((bf16[128,2,128]{2,1,0:T(2,128)(2,1)}), bf16[128,2,128]{2,1,0:T(2,128)(2,1)S(1)}, u32[]{:S(2)}, u32[]{:S(2)}) async-start(bf16[128,2,128]{2,1,0:T(2,128)(2,1)} %reshape.189), calls=%async_computation.2 | async-start | bytes 131072 | tf_op jit(solution)/shard_map/all_to_all | solution.py:98
  81.6 32.2 %copy-start.5 = (bf16[256,64]{0,1:T(8,128)(2,1)S(1)}, bf16[256,64]{0,1:T(8,128)(2,1)}, u32[]{:S(2)}) copy-start(bf16[256,64]{0,1:T(8,128)(2,1)} %param.12) | copy-start | bytes 98308
  81.6 32.2 %copy-start.6 = (f32[64]{0:T(128)S(1)}, f32[64]{0:T(128)}, u32[]{:S(2)}) copy-start(f32[64]{0:T(128)} %param.13) | copy-start | bytes 772
  107.2 11.6 %all-to-all-start.3 = ((bf16[8,2,2048]{2,1,0:T(2,128)(2,1)}), bf16[8,2,2048]{2,1,0:T(2,128)(2,1)S(1)}, u32[]{:S(2)}, u32[]{:S(2)}) async-start(bf16[8,2,2048]{2,1,0:T(2,128)(2,1)} %reshape.191), calls=%async_computation.3 | async-start | bytes 131072 | tf_op jit(solution)/shard_map/all_to_all | solution.py:66
  113.9 5.3 %copy-start.4 = (bf16[1,2,24,64,128]{4,3,2,1,0:T(8,128)(2,1)S(1)}, bf16[1,2,24,64,128]{4,3,2,1,0:T(8,128)(2,1)}, u32[]{:S(2)}) copy-start(bf16[1,2,24,64,128]{4,3,2,1,0:T(8,128)(2,1)} %param.8) | copy-start | bytes 2359300
  196.3 11.6 %all-to-all-start.7 = ((bf16[8,2,2048]{2,1,0:T(2,128)(2,1)}), bf16[8,2,2048]{2,1,0:T(2,128)(2,1)S(1)}, u32[]{:S(2)}, u32[]{:S(2)}) async-start(bf16[8,2,2048]{2,1,0:T(2,128)(2,1)} %reshape.199), calls=%async_computation.7 | async-start | bytes 131072 | tf_op jit(solution)/shard_map/all_to_all | solution.py:66

commit v6 on v5

--- a/solution.py
+++ b/solution.py
@@ -122,9 +122,8 @@
     grad_weight = (bdot("bjgc,bjgo->jgco", routed, grad_routed) * factor).reshape(
         local_modes, group_modes, C * C
     )
-    grad_field = (bdot("bxyhz,ch->bxycz", grad_act, w_in) + synthesise(back_routed)).astype(
-        jnp.bfloat16
-    )
+    channel_grad = lax.optimization_barrier(bdot("bxyhz,ch->bxycz", grad_act, w_in))
+    grad_field = (channel_grad + synthesise(back_routed)).astype(jnp.bfloat16)
     return (grad_field, grad_weight)
 
 

time: 216 us -> 211 us (0.977)
  blocking collectives: 71.1 us -> 40.2 us
  waiting for transfers between devices: 54.3 us -> 72.6 us
  starting transfers between devices: 59 us -> 65.7 us
    all_to_all x1 -> x0, blocking collectives: 30.9 us -> none  [synthesise(): lax.all_to_all(sent, owners, split_axis=0, concat_axis=0, tiled=True)]
    all_to_all x1 -> x2, waiting for transfers between devices: 20.7 us -> 38.9 us  [synthesise(): lax.all_to_all(sent, owners, split_axis=0, concat_axis=0, tiled=True)]
    all_to_all x1 -> x2, starting transfers between devices: 6.95 us -> 13.6 us  [synthesise(): lax.all_to_all(sent, owners, split_axis=0, concat_axis=0, tiled=True)]
  transfers between devices with their start and end apart: 5 -> 6, of which waited for: 5 -> 6; matrix products, arithmetic and copies ran while one was open for 4% -> 7% of each run, Pallas kernels for 0% -> 0%
where the time goes in v6:
time: 211 us; the launch traced here: 210 us
  waiting for transfers between devices  72.6 us (34%)
  starting transfers between devices  65.7 us (31%)
  blocking collectives  40.2 us (19%)
  matrix products  21.7 us (10%)
  local copies, waits for them, and re-layouts  8.29 us (4%)
    all_to_all x2, waiting for transfers between devices, synthesise(): lax.all_to_all(sent, owners, split_axis=0, concat_axis=0, tiled=True)  38.9 us
    all_to_all x1, blocking collectives, analyse(): lax.all_to_all(ordered, owners, split_axis=0, concat_axis=0, tiled=True)  31 us
    all_to_all x1, waiting for transfers between devices, analyse(): lax.all_to_all(ordered, owners, split_axis=0, concat_axis=0, tiled=True)  24.7 us
    dot_general x18, matrix products, bdot(): return jnp.einsum(form, left, right, preferred_element_type=jnp.float32)  21.7 us
    all_to_all x1, starting transfers between devices, analyse(): lax.all_to_all(ordered, owners, split_axis=0, concat_axis=0, tiled=True)  21.3 us
    all_to_all x1, starting transfers between devices, gather_inner(): return lax.all_to_all(local, 'yc', split_axis=2, concat_axis=1, tiled=True)  17.4 us
    all_to_all x2, starting transfers between devices, synthesise(): lax.all_to_all(sent, owners, split_axis=0, concat_axis=0, tiled=True)  13.6 us
    all_to_all x2, starting transfers between devices, scatter_inner(): whole = lax.all_to_all(whole, 'yc', split_axis=1, concat_axis=2, tiled=True)  13.4 us
  transfers between devices with their start and end apart: 6, of which 6 were waited for; matrix products, arithmetic and copies ran while one was open for 7% of the time, Pallas kernels for 0%

profile of v6, /device:TPU:1, one launch (start us, length us, event | category | flops | bytes accessed | tf_op | source)
XLA Modules:
  0.0 210.3 jit_solution(342529544113123975)
XLA Ops:
  2.7 0.8 reshape.185
  3.5 17.4 %all-to-all-start = ((bf16[8,2,2048]{2,1,0:T(2,128)(2,1)}), bf16[8,2,2048]{2,1,0:T(2,128)(2,1)S(1)}, u32[]{:S(2)}, u32[]{:S(2)}) async-start(bf16[8,2,2048]{2,1,0:T(2,128)(2,1)} %reshape.185), calls=%async_computation | async-start | bytes 131072 | tf_op jit(solution)/shard_map/all_to_all | solution.py:63
  21.1 4.6 %all-to-all-done = bf16[8,2,2048]{2,1,0:T(2,128)(2,1)S(1)} async-done(((bf16[8,2,2048]{2,1,0:T(2,128)(2,1)}), bf16[8,2,2048]{2,1,0:T(2,128)(2,1)S(1)}, u32[]{:S(2)}, u32[]{:S(2)}) %all-to-all-start) | async-done | bytes 65568 | tf_op jit(solution)/shard_map/all_to_all | solution.py:63
  26.3 0.7 reshape.187
  27.0 21.3 %all-to-all-start.1 = ((bf16[128,2,128]{2,1,0:T(2,128)(2,1)}), bf16[128,2,128]{2,1,0:T(2,128)(2,1)S(1)}, u32[]{:S(2)}, u32[]{:S(2)}) async-start(bf16[128,2,128]{2,1,0:T(2,128)(2,1)} %reshape.187), calls=%async_computation.1 | async-start | bytes 131072 | tf_op jit(solution)/shard_map/all_to_all | solution.py:85
  48.5 24.7 %all-to-all-done.1 = bf16[128,2,128]{2,1,0:T(2,128)(2,1)S(1)} async-done(((bf16[128,2,128]{2,1,0:T(2,128)(2,1)}), bf16[128,2,128]{2,1,0:T(2,128)(2,1)S(1)}, u32[]{:S(2)}, u32[]{:S(2)}) %all-to-all-start.1) | async-done | bytes 65568 | tf_op jit(solution)/shard_map/all_to_all | solution.py:85
  73.9 0.7 reshape.189
  74.6 7.0 %all-to-all-start.2 = ((bf16[128,2,128]{2,1,0:T(2,128)(2,1)}), bf16[128,2,128]{2,1,0:T(2,128)(2,1)S(1)}, u32[]{:S(2)}, u32[]{:S(2)}) async-start(bf16[128,2,128]{2,1,0:T(2,128)(2,1)} %reshape.189), calls=%async_computation.2 | async-start | bytes 131072 | tf_op jit(solution)/shard_map/all_to_all | solution.py:98
  81.6 3.7 %fusion.6 = f32[1,2,24,256,128]{4,3,2,1,0:T(8,128)} fusion(f32[256]{0:T(256)S(1)} %copy-done.3, bf16[1,2,24,64,128]{4,3,2,1,0:T(8,128)(2,1)S(1)} %copy-done, bf16[64,256]{1,0:T(8,128)(2,1)S(1)} %copy-done.1), kind=kOutput, calls=%fused_computation.8 | convolution fusion | flops 202899456 | bytes 7111680 | tf_op jit(solution)/shard_map/bxycz,ch->bxyhz/dot_general | solution.py:43
  85.3 20.7 %all-to-all-done.2 = bf16[128,2,128]{2,1,0:T(2,128)(2,1)S(1)} async-done(((bf16[128,2,128]{2,1,0:T(2,128)(2,1)}), bf16[128,2,128]{2,1,0:T(2,128)(2,1)S(1)}, u32[]{:S(2)}, u32[]{:S(2)}) %all-to-all-start.2) | async-done | bytes 65568 | tf_op jit(solution)/shard_map/all_to_all | solution.py:98
  106.4 0.8 reshape.191
  107.2 6.7 %all-to-all-start.3 = ((bf16[8,2,2048]{2,1,0:T(2,128)(2,1)}), bf16[8,2,2048]{2,1,0:T(2,128)(2,1)S(1)}, u32[]{:S(2)}, u32[]{:S(2)}) async-start(bf16[8,2,2048]{2,1,0:T(2,128)(2,1)} %reshape.191), calls=%async_computation.3 | async-start | bytes 131072 | tf_op jit(solution)/shard_map/all_to_all | solution.py:66
  113.9 4.6 %fusion.20 = f32[1,2,24,64,128]{4,3,2,1,0:T(8,128)} fusion(f32[1,2,24,256,128]{4,3,2,1,0:T(8,128)} %fusion.6, f32[64]{0:T(128)S(1)} %copy-done.6, bf16[256,64]{0,1:T(8,128)(2,1)S(1)} %copy-done.5), kind=kOutput, calls=%fused_computation.23 | convolution fusion | flops 209584128 | bytes 7897344 | tf_op jit(solution)/shard_map/bxyhz,hc->bxycz/dot_general | solution.py:43
  119.1 2.5 %fusion.27 = bf16[2,24,64,128]{3,2,1,0:T(8,128)(2,1)S(1)} fusion(f32[1,2,24,64,128]{4,3,2,1,0:T(8,128)} %fusion.20, bf16[1,2,24,64,128]{4,3,2,1,0:T(8,128)(2,1)S(1)} %copy-done.4, bf16[2,24,64,16]{2,1,3,0:T(8,128)(2,1)S(1)} %fusion.29, bf16[8,128]{1,0:T(8,128)(2,1)S(1)} %get-tuple-element.9, bf16[8,128]{1,0:T(8,128)(2,1)S(1)} %get-tuple-element.8), kind=kOutput, calls=%fused_computation.28 | convolution fusion | flops 17702912 | bytes 3248128 | tf_op jit(solution)/shard_map/bxyck,kz->bxycz/dot_general | solution.py:43
  122.7 9.2 %all_to_all.74 = bf16[8,2,2048]{2,1,0:T(2,128)(2,1)S(1)} all-to-all(bf16[8,2,2048]{2,1,0:T(2,128)(2,1)S(1)} %reshape.193), channel_id=1, replica_groups=mesh['zh'=2,'yc'=8,'dp'=64] {'yc'}, dimensions={0} | all-to-all | bytes 131072 | tf_op jit(solution)/shard_map/all_to_all | solution.py:63
  132.6 31.0 %all_to_all.75 = bf16[128,2,128]{2,1,0:T(2,128)(2,1)S(1)} all-to-all(bf16[128,2,128]{2,1,0:T(2,128)(2,1)S(1)} %reshape.195), channel_id=1, replica_groups=mesh['zh'=2,'yc'=8,'dp'=64] {'zh','dp'}, dimensions={0} | all-to-all | bytes 131072 | tf_op jit(solution)/shard_map/all_to_all | solution.py:85
  164.1 0.7 reshape.197
  164.8 6.6 %all-to-all-start.6 = ((bf16[128,2,128]{2,1,0:T(2,128)(2,1)}), bf16[128,2,128]{2,1,0:T(2,128)(2,1)S(1)}, u32[]{:S(2)}, u32[]{:S(2)}) async-start(bf16[128,2,128]{2,1,0:T(2,128)(2,1)} %reshape.197), calls=%async_computation.6 | async-start | bytes 131072 | tf_op jit(solution)/shard_map/all_to_all | solution.py:98
  171.5 6.1 %fusion.22 = f32[1,2,24,64,128]{4,3,2,1,0:T(8,128)S(1)} fusion(f32[1,2,24,256,128]{4,3,2,1,0:T(8,128)} %fusion.6, bf16[2,24,64,128]{3,2,1,0:T(8,128)(2,1)S(1)} %fusion.27, bf16[256,64]{0,1:T(8,128)(2,1)S(1)} %copy-done.5, bf16[64,256]{1,0:T(8,128)(2,1)S(1)} %copy-done.1), kind=kOutput, calls=%fused_computation.27 | convolution fusion | flops 418381824 | bytes 8716288 | tf_op jit(solution)/shard_map/bxyhz,ch->bxycz/dot_general | solution.py:43
  177.6 18.3 %all-to-all-done.6 = bf16[128,2,128]{2,1,0:T(2,128)(2,1)S(1)} async-done(((bf16[128,2,128]{2,1,0:T(2,128)(2,1)}), bf16[128,2,128]{2,1,0:T(2,128)(2,1)S(1)}, u32[]{:S(2)}, u32[]{:S(2)}) %all-to-all-start.6) | async-done | bytes 65568 | tf_op jit(solution)/shard_map/all_to_all | solution.py:98
  196.2 0.8 reshape.199
  197.0 6.7 %all-to-all-start.7 = ((bf16[8,2,2048]{2,1,0:T(2,128)(2,1)}), bf16[8,2,2048]{2,1,0:T(2,128)(2,1)S(1)}, u32[]{:S(2)}, u32[]{:S(2)}) async-start(bf16[8,2,2048]{2,1,0:T(2,128)(2,1)} %reshape.199), calls=%async_computation.7 | async-start | bytes 131072 | tf_op jit(solution)/shard_map/all_to_all | solution.py:66
  204.6 4.0 %all-to-all-done.7 = bf16[8,2,2048]{2,1,0:T(2,128)(2,1)S(1)} async-done(((bf16[8,2,2048]{2,1,0:T(2,128)(2,1)}), bf16[8,2,2048]{2,1,0:T(2,128)(2,1)S(1)}, u32[]{:S(2)}, u32[]{:S(2)}) %all-to-all-start.7) | async-done | bytes 65568 | tf_op jit(solution)/shard_map/all_to_all | solution.py:66
  209.0 1.3 fusion.21
  (69 shorter events, 8.3 us)
Async XLA Ops:
  0.6 1.1 copy-start
  0.6 47.7 %copy-start.2 = (bf16[1,4,4096]{2,1,0:T(4,128)(2,1)S(1)}, bf16[1,4,4096]{2,1,0:T(4,128)(2,1)}, u32[]{:S(2)}) copy-start(bf16[1,4,4096]{2,1,0:T(4,128)(2,1)} %param.9) | copy-start | bytes 98308
  0.7 80.9 %copy-start.1 = (bf16[64,256]{1,0:T(8,128)(2,1)S(1)}, bf16[64,256]{1,0:T(8,128)(2,1)}, u32[]{:S(2)}) copy-start(bf16[64,256]{1,0:T(8,128)(2,1)} %param.10) | copy-start | bytes 98308
  0.7 80.9 %copy-start.3 = (f32[256]{0:T(256)S(1)}, f32[256]{0:T(256)}, u32[]{:S(2)}) copy-start(f32[256]{0:T(256)} %param.11) | copy-start | bytes 3076
  3.5 22.2 %all-to-all-start = ((bf16[8,2,2048]{2,1,0:T(2,128)(2,1)}), bf16[8,2,2048]{2,1,0:T(2,128)(2,1)S(1)}, u32[]{:S(2)}, u32[]{:S(2)}) async-start(bf16[8,2,2048]{2,1,0:T(2,128)(2,1)} %reshape.185), calls=%async_computation | async-start | bytes 131072 | tf_op jit(solution)/shard_map/all_to_all | solution.py:63
  27.0 46.2 %all-to-all-start.1 = ((bf16[128,2,128]{2,1,0:T(2,128)(2,1)}), bf16[128,2,128]{2,1,0:T(2,128)(2,1)S(1)}, u32[]{:S(2)}, u32[]{:S(2)}) async-start(bf16[128,2,128]{2,1,0:T(2,128)(2,1)} %reshape.187), calls=%async_computation.1 | async-start | bytes 131072 | tf_op jit(solution)/shard_map/all_to_all | solution.py:85
  74.6 31.4 %all-to-all-start.2 = ((bf16[128,2,128]{2,1,0:T(2,128)(2,1)}), bf16[128,2,128]{2,1,0:T(2,128)(2,1)S(1)}, u32[]{:S(2)}, u32[]{:S(2)}) async-start(bf16[128,2,128]{2,1,0:T(2,128)(2,1)} %reshape.189), calls=%async_computation.2 | async-start | bytes 131072 | tf_op jit(solution)/shard_map/all_to_all | solution.py:98
  81.6 32.2 %copy-start.5 = (bf16[256,64]{0,1:T(8,128)(2,1)S(1)}, bf16[256,64]{0,1:T(8,128)(2,1)}, u32[]{:S(2)}) copy-start(bf16[256,64]{0,1:T(8,128)(2,1)} %param.12) | copy-start | bytes 98308
  81.6 32.2 %copy-start.6 = (f32[64]{0:T(128)S(1)}, f32[64]{0:T(128)}, u32[]{:S(2)}) copy-start(f32[64]{0:T(128)} %param.13) | copy-start | bytes 772
  107.2 11.6 %all-to-all-start.3 = ((bf16[8,2,2048]{2,1,0:T(2,128)(2,1)}), bf16[8,2,2048]{2,1,0:T(2,128)(2,1)S(1)}, u32[]{:S(2)}, u32[]{:S(2)}) async-start(bf16[8,2,2048]{2,1,0:T(2,128)(2,1)} %reshape.191), calls=%async_computation.3 | async-start | bytes 131072 | tf_op jit(solution)/shard_map/all_to_all | solution.py:66
  113.9 5.3 %copy-start.4 = (bf16[1,2,24,64,128]{4,3,2,1,0:T(8,128)(2,1)S(1)}, bf16[1,2,24,64,128]{4,3,2,1,0:T(8,128)(2,1)}, u32[]{:S(2)}) copy-start(bf16[1,2,24,64,128]{4,3,2,1,0:T(8,128)(2,1)} %param.8) | copy-start | bytes 2359300
  164.8 31.0 %all-to-all-start.6 = ((bf16[128,2,128]{2,1,0:T(2,128)(2,1)}), bf16[128,2,128]{2,1,0:T(2,128)(2,1)S(1)}, u32[]{:S(2)}, u32[]{:S(2)}) async-start(bf16[128,2,128]{2,1,0:T(2,128)(2,1)} %reshape.197), calls=%async_computation.6 | async-start | bytes 131072 | tf_op jit(solution)/shard_map/all_to_all | solution.py:98
  197.0 11.6 %all-to-all-start.7 = ((bf16[8,2,2048]{2,1,0:T(2,128)(2,1)}), bf16[8,2,2048]{2,1,0:T(2,128)(2,1)S(1)}, u32[]{:S(2)}, u32[]{:S(2)}) async-start(bf16[8,2,2048]{2,1,0:T(2,128)(2,1)} %reshape.199), calls=%async_computation.7 | async-start | bytes 131072 | tf_op jit(solution)/shard_map/all_to_all | solution.py:66
